TPU v7x, 256 devices: a whole 4x4x8 slice. The times are simulated.
256 devices in a mesh: wide: 16 (over z, core), narrow: 16 (over x, y).
Axes of the slice: x: 4, y: 4, z: 8, core: 2. Of those that a mesh axis runs over, the one named last changes fastest.
Arguments:
- source: float32 [256, 2048, 128], P('wide', 'narrow'), may hold values from -14 to 14, as said below
- reaction: float32 [256, 2048, 128], P('wide', 'narrow'), may hold values from 0.02 to 0.2
- conductance: float32 [256, 2048, 128], P('wide', 'narrow'), may hold values from 0.25 to 2
- coarse_inverse: float32 [16, 16, 8, 2048], P('wide', 'narrow'), may hold values from -1 to 16, as said below
Outputs:
- solution: float32 [256, 2048, 128], P('wide', 'narrow')
- residual: float32 [256, 2048, 128], P('wide', 'narrow')
- direction: float32 [256, 2048, 128], P('wide', 'narrow')
Inputs may be any that keep to these rules, and one draw needn't show every extreme that they name: source: finite values of either sign. coarse_inverse: a symmetric positive definite matrix.
All inputs are finite; a program needn't handle non-finite values.
Results may differ from a plain program's by a relative error of at most 0.0003.
Values sent between devices are 32-bit elements; how exact they have to be, the bound alone decides.
No kernel may reach another device: no remote copies, remote signals or barrier semaphores. Data moves between devices by JAX's collectives and lax.ppermute only.
A program may use at most 64 MiB of HBM per device.

v0:
```python
import jax
import jax.numpy as jnp
from jax import lax
from jax.sharding import PartitionSpec as P

W = 8
PRIMAL = 8
ITERS = 2


SHIFT = 0.06
KAPPA = 1.0


def with_halo(block, sides, width):
    for axis, dim in sides:
        count = lax.axis_size(axis)
        forward = [(i, i + 1) for i in range(count - 1)]
        backward = [(target, source) for source, target in forward]
        low = lax.ppermute(
            lax.slice_in_dim(block, block.shape[dim] - width, None, axis=dim), axis, forward
        )
        high = lax.ppermute(lax.slice_in_dim(block, 0, width, axis=dim), axis, backward)
        block = jnp.concatenate([low, block, high], axis=dim)
    return block


def passed_along(block, axis, distance):
    devices = range(lax.axis_size(axis))
    route = [(i - distance, i) for i in devices if i - distance in devices]
    return lax.ppermute(block, axis, route)


def sine_basis(extent):
    indices = jnp.arange(extent, dtype=jnp.float32) + 1.0
    angles = jnp.pi * indices[:, None] * indices[None, :] / (extent + 1)
    sine_table = jnp.sqrt(2.0 / (extent + 1)) * jnp.sin(angles)
    eigenvalues = 2.0 - 2.0 * jnp.cos(jnp.pi * indices / (extent + 1))
    return (sine_table, eigenvalues)


def harmonic(first, second):
    return 2.0 * first * second / (first + second)


def face_weights(padded_cond, conductance):
    face_x = harmonic(padded_cond[:-1, 1:-1], padded_cond[1:, 1:-1])
    face_y = harmonic(padded_cond[1:-1, :-1], padded_cond[1:-1, 1:])
    face_z = harmonic(conductance[:, :, :-1], conductance[:, :, 1:])
    return (face_x, face_y, face_z)


def operate(field, padded_field, reaction, face_x, face_y, face_z):
    result = reaction * field
    result = (
        result
        + face_x[1:] * (field - padded_field[2:, 1:-1])
        + face_x[:-1] * (field - padded_field[:-2, 1:-1])
    )
    result = (
        result
        + face_y[:, 1:] * (field - padded_field[1:-1, 2:])
        + face_y[:, :-1] * (field - padded_field[1:-1, :-2])
    )
    flux_z = face_z * (field[:, :, :-1] - field[:, :, 1:])
    return (
        result
        + jnp.pad(flux_z, ((0, 0), (0, 0), (0, 1)))
        - jnp.pad(flux_z, ((0, 0), (0, 0), (1, 0)))
    )


def transform_first(field, table_x):
    return jnp.einsum("ryz,re->eyz", field, table_x, precision=lax.Precision.HIGHEST)


def transform_cross(field, table_y, table_z):
    inner = jnp.einsum("ryz,zc->ryc", field, table_z, precision=lax.Precision.HIGHEST)
    return jnp.einsum("ryc,yb->rbc", inner, table_y, precision=lax.Precision.HIGHEST)


def body(source, reaction, conductance, coarse_inverse):
    block_x, block_y, block_z = source.shape
    extended = block_x + 2 * W
    padded_cond = with_halo(conductance, (("wide", 0), ("narrow", 1)), 1)
    face_x, face_y, face_z = face_weights(padded_cond, conductance)
    table_x, eigen_x = sine_basis(extended)
    table_y, eigen_y = sine_basis(block_y)
    table_z, eigen_z = sine_basis(block_z)
    spectrum = SHIFT + KAPPA * (
        eigen_x[:, None, None] + eigen_y[None, :, None] + eigen_z[None, None, :]
    )
    coarse_rows = coarse_inverse.reshape(PRIMAL, -1)

    def widen(field):
        return with_halo(field, (("wide", 0),), W)

    def fold_back(solved):
        owned = solved[W : W + block_x]
        for offset in (1, -1):
            rim_piece = solved[W + block_x :] if offset == 1 else solved[:W]
            arrived = passed_along(rim_piece, "wide", offset)
            if offset == 1:
                owned = owned + jnp.pad(arrived, ((0, block_x - W), (0, 0), (0, 0)))
            else:
                owned = owned + jnp.pad(arrived, ((block_x - W, 0), (0, 0), (0, 0)))
        return owned

    def precondition(field):
        coeffs = (
            transform_cross(transform_first(widen(field), table_x), table_y, table_z) / spectrum
        )
        local_part = fold_back(transform_cross(transform_first(coeffs, table_x), table_y, table_z))
        octant_means = (
            field.reshape(2, block_x // 2, 2, block_y // 2, 2, block_z // 2)
            .mean(axis=(1, 3, 5))
            .reshape(PRIMAL)
        )
        all_means = lax.all_gather(octant_means, ("wide", "narrow"), axis=0, tiled=True)
        correction = jnp.dot(coarse_rows, all_means, precision=lax.Precision.HIGHEST).reshape(
            2, 2, 2
        )
        spread = jnp.broadcast_to(
            correction[:, None, :, None, :, None],
            (2, block_x // 2, 2, block_y // 2, 2, block_z // 2),
        )
        return local_part + spread.reshape(block_x, block_y, block_z)

    def inner_norm(residual, preconditioned):
        return lax.psum(jnp.sum(residual * preconditioned), ("wide", "narrow"))

    solution = jnp.zeros_like(source)
    residual = source
    preconditioned = precondition(residual)
    direction = preconditioned
    gamma_now = inner_norm(residual, preconditioned)
    for iteration in range(ITERS):
        padded_field = with_halo(direction, (("wide", 0), ("narrow", 1)), 1)
        image = operate(direction, padded_field, reaction, face_x, face_y, face_z)
        step_size = gamma_now / lax.psum(jnp.sum(direction * image), ("wide", "narrow"))
        solution = solution + step_size * direction
        residual = residual - step_size * image
        preconditioned = precondition(residual)
        gamma_next = inner_norm(residual, preconditioned)
        direction = preconditioned + gamma_next / gamma_now * direction
        gamma_now = gamma_next
    return (solution, residual, direction)


def solution(mesh):
    in_specs = (
        P("wide", "narrow", None),
        P("wide", "narrow", None),
        P("wide", "narrow", None),
        P("wide", "narrow", None, None),
    )
    out_specs = (P("wide", "narrow", None), P("wide", "narrow", None), P("wide", "narrow", None))
    return jax.shard_map(body, mesh=mesh, in_specs=in_specs, out_specs=out_specs, check_vma=False)
```

profile of v0, /device:TPU:32, one launch (start us, length us, event | category | flops | bytes accessed | tf_op | source)
XLA Modules:
  0.0 757.5 jit_solution(6966355934490457965)
XLA Ops:
  19.5 80.1 %all-reduce.10 = f32[2048]{0:T(1024)S(1)} all-reduce(f32[2048]{0:T(1024)S(1)} %dynamic-update-slice), channel_id=1, replica_groups=mesh['wide'=16,'narrow'=16] {'wide','narrow'}, use_global_device_ids=true, to_apply=%add.10 | all-reduce | flops 2048 | bytes 16384
  103.4 3.5 reshape.123
  112.0 3.7 fusion.20
  121.3 3.7 fusion.17
  133.1 4.5 collective-permute-start.8
  151.7 3.6 collective-permute-done.10
  158.6 78.9 %all-reduce.13 = (f32[]{:T(128)}, f32[]{:T(128)}) all-reduce(f32[]{:T(128)} %get-tuple-element.4, f32[]{:T(128)} %get-tuple-element.3), channel_id=1, replica_groups=mesh['wide'=16,'narrow'=16] {'wide','narrow'}, use_global_device_ids=true, to_apply=%region_2.3 | all-reduce | flops 2 | bytes 16 | tf_op jit(solution)/shard_map/psum | solution.py:130
  245.1 3.9 collective-permute-done.13
  249.0 3.8 collective-permute-done.12
  256.1 3.7 fusion.13
  265.4 3.7 fusion.10
  269.1 3.5 convolution_bitcast_fusion.1
  284.7 75.8 %all-reduce.11 = f32[2048]{0:T(1024)S(1)} all-reduce(f32[2048]{0:T(1024)S(1)} %dynamic-update-slice.1), channel_id=1, replica_groups=mesh['wide'=16,'narrow'=16] {'wide','narrow'}, use_global_device_ids=true, to_apply=%add.11 | all-reduce | flops 2048 | bytes 16384
  369.7 74.5 %psum.37 = f32[]{:T(128)} all-reduce(f32[]{:T(128)} %multiply_reduce_fusion.2), channel_id=1, replica_groups=mesh['wide'=16,'narrow'=16] {'wide','narrow'}, use_global_device_ids=true, to_apply=%region_7.8 | all-reduce | flops 1 | bytes 8 | tf_op jit(solution)/shard_map/psum | solution.py:130
  460.8 3.6 collective-permute-done.18
  467.5 77.2 %psum.38 = f32[]{:T(128)} all-reduce(f32[]{:T(128)} %get-tuple-element.7), channel_id=1, replica_groups=mesh['wide'=16,'narrow'=16] {'wide','narrow'}, use_global_device_ids=true, to_apply=%region_9.10 | all-reduce | flops 1 | bytes 8 | tf_op jit(solution)/shard_map/psum | solution.py:140
  552.2 3.9 collective-permute-done.21
  556.1 3.8 collective-permute-done.20
  563.3 3.7 fusion.6
  572.6 3.7 fusion.3
  576.3 3.5 convolution_bitcast_fusion
  592.1 75.7 %all-reduce.12 = f32[2048]{0:T(1024)S(1)} all-reduce(f32[2048]{0:T(1024)S(1)} %dynamic-update-slice.2), channel_id=1, replica_groups=mesh['wide'=16,'narrow'=16] {'wide','narrow'}, use_global_device_ids=true, to_apply=%add.12 | all-reduce | flops 2048 | bytes 16384
  677.6 74.7 %psum.39 = f32[]{:T(128)} all-reduce(f32[]{:T(128)} %multiply_reduce_fusion), channel_id=1, replica_groups=mesh['wide'=16,'narrow'=16] {'wide','narrow'}, use_global_device_ids=true, to_apply=%region_12.13 | all-reduce | flops 1 | bytes 8 | tf_op jit(solution)/shard_map/psum | solution.py:130
  753.6 3.6 multiply_add_fusion
  (152 shorter events, 150.2 us)
Async XLA Ops:
  2.1 105.4 %collective-permute-start.1 = (f32[8,128,128]{2,1,0:T(8,128)S(1)}, f32[8,128,128]{2,1,0:T(8,128)}, u32[]{:S(2)}, u32[]{:S(2)}) collective-permute-start(f32[8,128,128]{2,1,0:T(8,128)S(1)} %get-tuple-element.38), channel_id=1, source_target_pairs={{16,0},{32,16},{48,32},{64,48},{80,64},{96,80},{112,96},{128,112},... | collective-permute-start | bytes 1572872 | tf_op jit(solution)/shard_map/ppermute | solution.py:23
  4.0 103.5 %collective-permute-start = (f32[8,128,128]{2,1,0:T(8,128)S(1)}, f32[8,128,128]{2,1,0:T(8,128)}, u32[]{:S(2)}, u32[]{:S(2)}) collective-permute-start(f32[8,128,128]{2,1,0:T(8,128)S(1)} %get-tuple-element.37), channel_id=1, source_target_pairs={{0,16},{16,32},{32,48},{48,64},{64,80},{80,96},{96,112},{112,128},... | collective-permute-start | bytes 1572872 | tf_op jit(solution)/shard_map/ppermute | solution.py:20
  6.5 100.6 %collective-permute-start.4 = (f32[1,128,128]{2,1,0:T(8,128)S(1)}, f32[1,128,128]{2,1,0:T(8,128)S(1)}, u32[]{:S(2)}, u32[]{:S(2)}) collective-permute-start(f32[1,128,128]{2,1,0:T(8,128)S(1)} %get-tuple-element.34), channel_id=1, source_target_pairs={{0,16},{16,32},{32,48},{48,64},{64,80},{80,96},{96,112},{112,128},... | collective-permute-start | bytes 196616 | tf_op jit(solution)/shard_map/ppermute | solution.py:20
  9.9 97.5 %collective-permute-start.5 = (f32[1,128,128]{2,1,0:T(8,128)S(1)}, f32[1,128,128]{2,1,0:T(8,128)S(1)}, u32[]{:S(2)}, u32[]{:S(2)}) collective-permute-start(f32[1,128,128]{2,1,0:T(8,128)S(1)} %get-tuple-element.33), channel_id=1, source_target_pairs={{16,0},{32,16},{48,32},{64,48},{80,64},{96,80},{112,96},{128,112},... | collective-permute-start | bytes 196616 | tf_op jit(solution)/shard_map/ppermute | solution.py:23
  127.3 10.6 %collective-permute-start.3 = (f32[8,128,128]{2,1,0:T(8,128)S(1)}, f32[8,128,128]{2,1,0:T(8,128)S(1)}, u32[]{:S(2)}, u32[]{:S(2)}) collective-permute-start(f32[8,128,128]{2,1,0:T(8,128)S(1)} %get-tuple-element.15), channel_id=1, source_target_pairs={{16,0},{32,16},{48,32},{64,48},{80,64},{96,80},{112,96},{128,112},... | collective-permute-start | bytes 1572872 | tf_op jit(solution)/shard_map/ppermute | solution.py:31
  129.4 10.5 %collective-permute-start.2 = (f32[8,128,128]{2,1,0:T(8,128)S(1)}, f32[8,128,128]{2,1,0:T(8,128)S(1)}, u32[]{:S(2)}, u32[]{:S(2)}) collective-permute-start(f32[8,128,128]{2,1,0:T(8,128)S(1)} %get-tuple-element.14), channel_id=1, source_target_pairs={{0,16},{16,32},{32,48},{48,64},{64,80},{80,96},{96,112},{112,128},... | collective-permute-start | bytes 1572872 | tf_op jit(solution)/shard_map/ppermute | solution.py:31
  131.8 12.6 %collective-permute-start.9 = (f32[18,1,128]{2,1,0:T(1,128)S(1)}, f32[18,1,128]{2,1,0:T(1,128)S(1)}, u32[]{:S(2)}, u32[]{:S(2)}) collective-permute-start(f32[18,1,128]{2,1,0:T(1,128)S(1)} %get-tuple-element.21), channel_id=1, source_target_pairs={{1,0},{2,1},{3,2},{4,3},{5,4},{6,5},{7,6},{8,7},{9,8},{10,9},{11,1... | collective-permute-start | bytes 27656 | tf_op jit(solution)/shard_map/ppermute | solution.py:23
  133.1 11.3 %collective-permute-start.8 = (f32[18,1,128]{2,1,0:T(1,128)S(1)}, f32[18,1,128]{2,1,0:T(1,128)S(1)}, u32[]{:S(2)}, u32[]{:S(2)}) collective-permute-start(f32[18,1,128]{2,1,0:T(1,128)S(1)} %get-tuple-element.20), channel_id=1, source_target_pairs={{0,1},{1,2},{2,3},{3,4},{4,5},{5,6},{6,7},{7,8},{8,9},{9,10},{10,1... | collective-permute-start | bytes 27656 | tf_op jit(solution)/shard_map/ppermute | solution.py:20
  140.1 4.7 collective-permute-start.6
  142.0 5.6 collective-permute-start.7
  147.6 4.1 collective-permute-start.11
  149.7 5.7 collective-permute-start.10
  240.4 8.6 %collective-permute-start.13 = (f32[8,128,128]{2,1,0:T(8,128)S(1)}, f32[8,128,128]{2,1,0:T(8,128)S(1)}, u32[]{:S(2)}, u32[]{:S(2)}) collective-permute-start(f32[8,128,128]{2,1,0:T(8,128)S(1)} %get-tuple-element.29), channel_id=1, source_target_pairs={{16,0},{32,16},{48,32},{64,48},{80,64},{96,80},{112,96},{128,112},... | collective-permute-start | bytes 1572872 | tf_op jit(solution)/shard_map/ppermute | solution.py:23
  242.3 10.5 %collective-permute-start.12 = (f32[8,128,128]{2,1,0:T(8,128)S(1)}, f32[8,128,128]{2,1,0:T(8,128)S(1)}, u32[]{:S(2)}, u32[]{:S(2)}) collective-permute-start(f32[8,128,128]{2,1,0:T(8,128)S(1)} %get-tuple-element.28), channel_id=1, source_target_pairs={{0,16},{16,32},{32,48},{48,64},{64,80},{80,96},{96,112},{112,128},... | collective-permute-start | bytes 1572872 | tf_op jit(solution)/shard_map/ppermute | solution.py:20
  274.9 92.1 %collective-permute-start.15 = (f32[8,128,128]{2,1,0:T(8,128)}, f32[8,128,128]{2,1,0:T(8,128)}, u32[]{:S(2)}, u32[]{:S(2)}) collective-permute-start(f32[8,128,128]{2,1,0:T(8,128)} %get-tuple-element.13), channel_id=1, source_target_pairs={{16,0},{32,16},{48,32},{64,48},{80,64},{96,80},{112,96},{128,112},... | collective-permute-start | bytes 1572872 | tf_op jit(solution)/shard_map/ppermute | solution.py:31
  276.8 90.2 %collective-permute-start.14 = (f32[8,128,128]{2,1,0:T(8,128)}, f32[8,128,128]{2,1,0:T(8,128)}, u32[]{:S(2)}, u32[]{:S(2)}) collective-permute-start(f32[8,128,128]{2,1,0:T(8,128)} %get-tuple-element.12), channel_id=1, source_target_pairs={{0,16},{16,32},{32,48},{48,64},{64,80},{80,96},{96,112},{112,128},... | collective-permute-start | bytes 1572872 | tf_op jit(solution)/shard_map/ppermute | solution.py:31
  447.8 4.3 collective-permute-start.16
  449.8 5.6 collective-permute-start.17
  455.4 5.4 collective-permute-start.19
  458.6 5.8 collective-permute-start.18
  547.5 8.6 %collective-permute-start.21 = (f32[8,128,128]{2,1,0:T(8,128)S(1)}, f32[8,128,128]{2,1,0:T(8,128)S(1)}, u32[]{:S(2)}, u32[]{:S(2)}) collective-permute-start(f32[8,128,128]{2,1,0:T(8,128)S(1)} %get-tuple-element.25), channel_id=1, source_target_pairs={{16,0},{32,16},{48,32},{64,48},{80,64},{96,80},{112,96},{128,112},... | collective-permute-start | bytes 1572872 | tf_op jit(solution)/shard_map/ppermute | solution.py:23
  549.4 10.5 %collective-permute-start.20 = (f32[8,128,128]{2,1,0:T(8,128)S(1)}, f32[8,128,128]{2,1,0:T(8,128)S(1)}, u32[]{:S(2)}, u32[]{:S(2)}) collective-permute-start(f32[8,128,128]{2,1,0:T(8,128)S(1)} %get-tuple-element.24), channel_id=1, source_target_pairs={{0,16},{16,32},{32,48},{48,64},{64,80},{80,96},{96,112},{112,128},... | collective-permute-start | bytes 1572872 | tf_op jit(solution)/shard_map/ppermute | solution.py:20
  582.2 92.7 %collective-permute-start.23 = (f32[8,128,128]{2,1,0:T(8,128)}, f32[8,128,128]{2,1,0:T(8,128)}, u32[]{:S(2)}, u32[]{:S(2)}) collective-permute-start(f32[8,128,128]{2,1,0:T(8,128)} %get-tuple-element.11), channel_id=1, source_target_pairs={{16,0},{32,16},{48,32},{64,48},{80,64},{96,80},{112,96},{128,112},... | collective-permute-start | bytes 1572872 | tf_op jit(solution)/shard_map/ppermute | solution.py:31
  584.1 90.8 %collective-permute-start.22 = (f32[8,128,128]{2,1,0:T(8,128)}, f32[8,128,128]{2,1,0:T(8,128)}, u32[]{:S(2)}, u32[]{:S(2)}) collective-permute-start(f32[8,128,128]{2,1,0:T(8,128)} %get-tuple-element.10), channel_id=1, source_target_pairs={{0,16},{16,32},{32,48},{48,64},{64,80},{80,96},{96,112},{112,128},... | collective-permute-start | bytes 1572872 | tf_op jit(solution)/shard_map/ppermute | solution.py:31
  (19 other events, 379.2 us)
where the time goes:
time: 765 us; the launch traced here: 758 us
  blocking collectives  537 us (70%)
  matrix products  63 us (8%)
  starting transfers between devices  55.2 us (7%)
  other arithmetic  34.1 us (4%)
  waiting for transfers between devices  30.6 us (4%)
  local copies, waits for them, and re-layouts  30.5 us (4%)
    unnamed x3, blocking collectives  232 us
    psum x3, blocking collectives, inner_norm(): return lax.psum(jnp.sum(residual * preconditioned), ('wide', 'narrow'))  228 us
    psum x1, blocking collectives, body(): lax.psum(jnp.sum(direction * image), ('wide', 'narrow'))  77.2 us
    ppermute x9, starting transfers between devices, with_halo(): lax.ppermute(lax.slice_in_dim(block, block.shape[dim] - width, None, axis...  26 us
    dot_general x6, matrix products, transform_cross(): jnp.einsum('ryz,zc->ryc', field, table_z, precision=lax.Precision.HIGHEST)  22 us
    dot_general x6, matrix products, transform_first(): jnp.einsum('ryz,re->eyz', field, table_x, precision=lax.Precision.HIGHEST)  19.6 us
    ppermute x9, starting transfers between devices, with_halo(): lax.ppermute(lax.slice_in_dim(block, 0, width, axis=dim), axis, backward)  16.1 us
    dot_general x6, matrix products, transform_cross(): jnp.einsum('ryc,yb->rbc', inner, table_y, precision=lax.Precision.HIGHEST)  15.9 us
  transfers between devices with their start and end apart: 24, of which 9 were waited for; matrix products, arithmetic and copies ran while one was open for 5% of the time, Pallas kernels for 0%

commit v1 on v0

--- a/solution.py
+++ b/solution.py
@@ -29,6 +29,27 @@
     devices = range(lax.axis_size(axis))
     route = [(i - distance, i) for i in devices if i - distance in devices]
     return lax.ppermute(block, axis, route)
+
+
+def tree_sum(values):
+    while len(values) > 1:
+        values = [values[i] + values[i + 1] for i in range(0, len(values), 2)]
+    return values[0]
+
+
+def total_over(value, axes=("wide", "narrow"), radix=4):
+    for axis in axes:
+        count = lax.axis_size(axis)
+        stride = 1
+        while stride < count:
+            width = min(radix, count // stride)
+            pulled = [
+                lax.ppermute(value, axis, [(i, i ^ (j * stride)) for i in range(count)])
+                for j in range(1, width)
+            ]
+            value = tree_sum([value] + pulled)
+            stride *= width
+    return value
 
 
 def sine_basis(extent):
@@ -116,7 +137,11 @@
             .mean(axis=(1, 3, 5))
             .reshape(PRIMAL)
         )
-        all_means = lax.all_gather(octant_means, ("wide", "narrow"), axis=0, tiled=True)
+        slot = lax.axis_index("wide") * lax.axis_size("narrow") + lax.axis_index("narrow")
+        placed = lax.dynamic_update_slice(
+            jnp.zeros((coarse_rows.shape[1],), octant_means.dtype), octant_means, (slot * PRIMAL,)
+        )
+        all_means = total_over(placed)
         correction = jnp.dot(coarse_rows, all_means, precision=lax.Precision.HIGHEST).reshape(
             2, 2, 2
         )
@@ -127,17 +152,24 @@
         return local_part + spread.reshape(block_x, block_y, block_z)
 
     def inner_norm(residual, preconditioned):
-        return lax.psum(jnp.sum(residual * preconditioned), ("wide", "narrow"))
+        return total_over(jnp.sum(residual * preconditioned))
 
     solution = jnp.zeros_like(source)
     residual = source
     preconditioned = precondition(residual)
     direction = preconditioned
-    gamma_now = inner_norm(residual, preconditioned)
+    gamma_now = None
     for iteration in range(ITERS):
         padded_field = with_halo(direction, (("wide", 0), ("narrow", 1)), 1)
         image = operate(direction, padded_field, reaction, face_x, face_y, face_z)
-        step_size = gamma_now / lax.psum(jnp.sum(direction * image), ("wide", "narrow"))
+        if gamma_now is None:
+            both = total_over(
+                jnp.stack([jnp.sum(residual * preconditioned), jnp.sum(direction * image)])
+            )
+            gamma_now, curvature = both[0], both[1]
+        else:
+            curvature = total_over(jnp.sum(direction * image))
+        step_size = gamma_now / curvature
         solution = solution + step_size * direction
         residual = residual - step_size * image
         preconditioned = precondition(residual)

time: 765 us -> 468 us (0.61)
  blocking collectives: 537 us -> 0 us
  starting transfers between devices: 55.2 us -> 219 us
  waiting for transfers between devices: 30.6 us -> 68.2 us
  between operations: 7.08 us -> 29.6 us
  matrix products: 63 us -> 71.6 us
    psum x4 -> x0, blocking collectives: 305 us -> none  [the longest x3 228 us: inner_norm(): return lax.psum(jnp.sum(residual * preconditioned), ('wide', 'narrow'))]
    unnamed x3 -> x0, blocking collectives: 232 us -> none
    ppermute x0 -> x84, starting transfers between devices: none -> 163 us  [total_over(): lax.ppermute(value, axis, [(i, i ^ j * stride) for i in range(count)])]
    ppermute x0 -> x84, waiting for transfers between devices: none -> 52.7 us  [total_over(): lax.ppermute(value, axis, [(i, i ^ j * stride) for i in range(count)])]
    dot_general x6, matrix products: 19.6 us -> 28.3 us  [transform_first(): jnp.einsum('ryz,re->eyz', field, table_x, precision=lax.Precision.HIGHEST)]
    ppermute x9, waiting for transfers between devices: 15 us -> 7.25 us  [with_halo(): lax.ppermute(lax.slice_in_dim(block, 0, width, axis=dim), axis, backward)]
  transfers between devices with their start and end apart: 24 -> 108, of which waited for: 9 -> 45; matrix products, arithmetic and copies ran while one was open for 5% -> 15% of each run, Pallas kernels for 0% -> 0%
where the time goes in v1:
time: 468 us; the launch traced here: 459 us
  starting transfers between devices  219 us (47%)
  matrix products  71.6 us (15%)
  waiting for transfers between devices  68.2 us (15%)
  other arithmetic  38.4 us (8%)
  local copies, waits for them, and re-layouts  32.1 us (7%)
  between operations  29.6 us (6%)
    ppermute x84, starting transfers between devices, total_over(): lax.ppermute(value, axis, [(i, i ^ j * stride) for i in range(count)])  163 us
    ppermute x84, waiting for transfers between devices, total_over(): lax.ppermute(value, axis, [(i, i ^ j * stride) for i in range(count)])  52.7 us
    dot_general x6, matrix products, transform_first(): jnp.einsum('ryz,re->eyz', field, table_x, precision=lax.Precision.HIGHEST)  28.3 us
    dot_general x6, matrix products, transform_cross(): jnp.einsum('ryz,zc->ryc', field, table_z, precision=lax.Precision.HIGHEST)  22 us
    ppermute x9, starting transfers between devices, with_halo(): lax.ppermute(lax.slice_in_dim(block, block.shape[dim] - width, None, axis...  20.8 us
    ppermute x9, starting transfers between devices, with_halo(): lax.ppermute(lax.slice_in_dim(block, 0, width, axis=dim), axis, backward)  20.5 us
    dot_general x6, matrix products, transform_cross(): jnp.einsum('ryc,yb->rbc', inner, table_y, precision=lax.Precision.HIGHEST)  15.8 us
    ppermute x6, starting transfers between devices, passed_along(): return lax.ppermute(block, axis, route)  15.1 us
  transfers between devices with their start and end apart: 108, of which 45 were waited for; matrix products, arithmetic and copies ran while one was open for 15% of the time, Pallas kernels for 0%

profile of v1, /device:TPU:32, one launch (start us, length us, event | category | flops | bytes accessed | tf_op | source)
XLA Modules:
  0.0 459.0 jit_solution(14311247270664102591)
XLA Ops:
  9.3 3.6 collective-permute-start.1
  15.5 5.4 %collective-permute-start.8 = (f32[2048]{0:T(1024)S(1)}, f32[2048]{0:T(1024)S(1)}, u32[]{:S(2)}, u32[]{:S(2)}) collective-permute-start(f32[2048]{0:T(1024)S(1)} %add_add_fusion.15), channel_id=1, source_target_pairs={{0,128},{16,144},{32,160},{48,176},{64,192},{80,208},{96,224},{112... | collective-permute-start | bytes 24584 | tf_op jit(solution)/shard_map/ppermute | solution.py:47
  59.4 3.7 fusion.20
  65.3 12.1 %fusion.2 = f32[32,128,128]{2,0,1:T(8,128)S(1)} fusion(f32[128,32,128]{2,0,1:T(8,128)S(1)} %fusion.81, f32[128]{0:T(128)S(1)} %copy-done.18, f32[32,128]{0,1:T(8,128)S(1)} %broadcast_add_fusion, f32[32]{0:T(128)S(1)} %copy-done.15, f32[32]{0:T(128)S(1)} %copy-done.16), kind=kOutput, calls=%fused_computation.8 | convolution fusion | flops 202902528 | bytes 4211456 | tf_op jit(solution)/shard_map/ryz,re->eyz/dot_general | solution.py:95
  77.4 3.7 fusion.17
  89.2 4.5 collective-permute-start.20
  120.7 7.8 %collective-permute-start.28 = (f32[2]{0:T(128)S(1)}, f32[2]{0:T(128)S(1)}, u32[]{:S(2)}, u32[]{:S(2)}) collective-permute-start(f32[2]{0:T(128)S(1)} %add_add_fusion.19), channel_id=1, source_target_pairs={{0,128},{16,144},{32,160},{48,176},{64,192},{80,208},{96,224},{112... | collective-permute-start | bytes 32 | tf_op jit(solution)/shard_map/ppermute | solution.py:47
  130.0 4.1 collective-permute-done.29
  134.1 4.6 collective-permute-start.31
  183.3 3.7 fusion.13
  192.7 3.7 fusion.10
  202.1 4.4 collective-permute-start.39
  235.9 4.8 %collective-permute-start.57 = (f32[]{:T(128)}, f32[]{:T(128)}, u32[]{:S(2)}, u32[]{:S(2)}) collective-permute-start(f32[]{:T(128)} %add.572), channel_id=1, source_target_pairs={{0,192},{16,208},{32,224},{48,240},{64,128},{80,144},{96,160},{112... | collective-permute-start | bytes 20 | tf_op jit(solution)/shard_map/ppermute | solution.py:47
  258.1 3.8 collective-permute-start.62
  294.9 4.2 collective-permute-start.71
  299.1 4.4 collective-permute-start.72
  312.1 6.3 %collective-permute-start.75 = (f32[]{:T(128)}, f32[]{:T(128)}, u32[]{:S(2)}, u32[]{:S(2)}) collective-permute-start(f32[]{:T(128)} %add.593), channel_id=1, source_target_pairs={{0,2},{1,3},{2,0},{3,1},{4,6},{5,7},{6,4},{7,5},{8,10},{9,11},{10,... | collective-permute-start | bytes 20 | tf_op jit(solution)/shard_map/ppermute | solution.py:47
  327.0 4.4 collective-permute-start.78
  355.9 3.7 collective-permute-start.89
  371.0 3.7 fusion.6
  380.4 3.7 fusion.3
  419.5 5.3 %collective-permute-start.100 = (f32[]{:T(128)}, f32[]{:T(128)}, u32[]{:S(2)}, u32[]{:S(2)}) collective-permute-start(f32[]{:T(128)} %add.618), channel_id=1, source_target_pairs={{0,128},{16,144},{32,160},{48,176},{64,192},{80,208},{96,224},{112... | collective-permute-start | bytes 20 | tf_op jit(solution)/shard_map/ppermute | solution.py:47
  436.9 3.6 collective-permute-start.104
  454.8 3.8 multiply_add_fusion
  (334 shorter events, 316.5 us)
Async XLA Ops:
  9.3 45.5 %collective-permute-start.1 = (f32[8,128,128]{2,1,0:T(8,128)S(1)}, f32[8,128,128]{2,1,0:T(8,128)}, u32[]{:S(2)}, u32[]{:S(2)}) collective-permute-start(f32[8,128,128]{2,1,0:T(8,128)S(1)} %get-tuple-element.36), channel_id=1, source_target_pairs={{16,0},{32,16},{48,32},{64,48},{80,64},{96,80},{112,96},{128,112},... | collective-permute-start | bytes 1572872 | tf_op jit(solution)/shard_map/ppermute | solution.py:23
  13.0 41.9 %collective-permute-start = (f32[8,128,128]{2,1,0:T(8,128)S(1)}, f32[8,128,128]{2,1,0:T(8,128)}, u32[]{:S(2)}, u32[]{:S(2)}) collective-permute-start(f32[8,128,128]{2,1,0:T(8,128)S(1)} %get-tuple-element.35), channel_id=1, source_target_pairs={{0,16},{16,32},{32,48},{48,64},{64,80},{80,96},{96,112},{112,128},... | collective-permute-start | bytes 1572872 | tf_op jit(solution)/shard_map/ppermute | solution.py:20
  40.8 13.6 %collective-permute-start.16 = (f32[1,128,128]{2,1,0:T(8,128)S(1)}, f32[1,128,128]{2,1,0:T(8,128)S(1)}, u32[]{:S(2)}, u32[]{:S(2)}) collective-permute-start(f32[1,128,128]{2,1,0:T(8,128)S(1)} %get-tuple-element.32), channel_id=1, source_target_pairs={{0,16},{16,32},{32,48},{48,64},{64,80},{80,96},{96,112},{112,128},... | collective-permute-start | bytes 196616 | tf_op jit(solution)/shard_map/ppermute | solution.py:20
  43.0 11.8 %collective-permute-start.17 = (f32[1,128,128]{2,1,0:T(8,128)S(1)}, f32[1,128,128]{2,1,0:T(8,128)S(1)}, u32[]{:S(2)}, u32[]{:S(2)}) collective-permute-start(f32[1,128,128]{2,1,0:T(8,128)S(1)} %get-tuple-element.31), channel_id=1, source_target_pairs={{16,0},{32,16},{48,32},{64,48},{80,64},{96,80},{112,96},{128,112},... | collective-permute-start | bytes 196616 | tf_op jit(solution)/shard_map/ppermute | solution.py:23
  83.4 10.6 %collective-permute-start.3 = (f32[8,128,128]{2,1,0:T(8,128)S(1)}, f32[8,128,128]{2,1,0:T(8,128)S(1)}, u32[]{:S(2)}, u32[]{:S(2)}) collective-permute-start(f32[8,128,128]{2,1,0:T(8,128)S(1)} %get-tuple-element.13), channel_id=1, source_target_pairs={{16,0},{32,16},{48,32},{64,48},{80,64},{96,80},{112,96},{128,112},... | collective-permute-start | bytes 1572872 | tf_op jit(solution)/shard_map/ppermute | solution.py:31
  85.5 10.5 %collective-permute-start.2 = (f32[8,128,128]{2,1,0:T(8,128)S(1)}, f32[8,128,128]{2,1,0:T(8,128)S(1)}, u32[]{:S(2)}, u32[]{:S(2)}) collective-permute-start(f32[8,128,128]{2,1,0:T(8,128)S(1)} %get-tuple-element.12), channel_id=1, source_target_pairs={{0,16},{16,32},{32,48},{48,64},{64,80},{80,96},{96,112},{112,128},... | collective-permute-start | bytes 1572872 | tf_op jit(solution)/shard_map/ppermute | solution.py:31
  87.9 12.6 %collective-permute-start.21 = (f32[18,1,128]{2,1,0:T(1,128)S(1)}, f32[18,1,128]{2,1,0:T(1,128)S(1)}, u32[]{:S(2)}, u32[]{:S(2)}) collective-permute-start(f32[18,1,128]{2,1,0:T(1,128)S(1)} %get-tuple-element.19), channel_id=1, source_target_pairs={{1,0},{2,1},{3,2},{4,3},{5,4},{6,5},{7,6},{8,7},{9,8},{10,9},{11,1... | collective-permute-start | bytes 27656 | tf_op jit(solution)/shard_map/ppermute | solution.py:23
  89.2 11.3 %collective-permute-start.20 = (f32[18,1,128]{2,1,0:T(1,128)S(1)}, f32[18,1,128]{2,1,0:T(1,128)S(1)}, u32[]{:S(2)}, u32[]{:S(2)}) collective-permute-start(f32[18,1,128]{2,1,0:T(1,128)S(1)} %get-tuple-element.18), channel_id=1, source_target_pairs={{0,1},{1,2},{2,3},{3,4},{4,5},{5,6},{6,7},{7,8},{8,9},{9,10},{10,1... | collective-permute-start | bytes 27656 | tf_op jit(solution)/shard_map/ppermute | solution.py:20
  163.0 17.1 %collective-permute-start.37 = (f32[8,128,128]{2,1,0:T(8,128)S(1)}, f32[8,128,128]{2,1,0:T(8,128)S(1)}, u32[]{:S(2)}, u32[]{:S(2)}) collective-permute-start(f32[8,128,128]{2,1,0:T(8,128)S(1)} %get-tuple-element.27), channel_id=1, source_target_pairs={{16,0},{32,16},{48,32},{64,48},{80,64},{96,80},{112,96},{128,112},... | collective-permute-start | bytes 1572872 | tf_op jit(solution)/shard_map/ppermute | solution.py:23
  165.4 14.6 %collective-permute-start.36 = (f32[8,128,128]{2,1,0:T(8,128)S(1)}, f32[8,128,128]{2,1,0:T(8,128)S(1)}, u32[]{:S(2)}, u32[]{:S(2)}) collective-permute-start(f32[8,128,128]{2,1,0:T(8,128)S(1)} %get-tuple-element.26), channel_id=1, source_target_pairs={{0,16},{16,32},{32,48},{48,64},{64,80},{80,96},{96,112},{112,128},... | collective-permute-start | bytes 1572872 | tf_op jit(solution)/shard_map/ppermute | solution.py:20
  176.0 32.4 %collective-permute-start.47 = (f32[2048]{0:T(1024)S(1)}, f32[2048]{0:T(1024)S(1)}, u32[]{:S(2)}, u32[]{:S(2)}) collective-permute-start(f32[2048]{0:T(1024)S(1)} %add_add_fusion.10), channel_id=1, source_target_pairs={{0,2},{1,3},{2,0},{3,1},{4,6},{5,7},{6,4},{7,5},{8,10},{9,11},{10,... | collective-permute-start | bytes 24584 | tf_op jit(solution)/shard_map/ppermute | solution.py:47
  178.9 29.5 %collective-permute-start.48 = (f32[2048]{0:T(1024)S(1)}, f32[2048]{0:T(1024)S(1)}, u32[]{:S(2)}, u32[]{:S(2)}) collective-permute-start(f32[2048]{0:T(1024)S(1)} %add_add_fusion.10), channel_id=1, source_target_pairs={{0,3},{1,2},{2,1},{3,0},{4,7},{5,6},{6,5},{7,4},{8,11},{9,10},{10,... | collective-permute-start | bytes 24584 | tf_op jit(solution)/shard_map/ppermute | solution.py:47
  179.6 28.8 %collective-permute-start.46 = (f32[2048]{0:T(1024)S(1)}, f32[2048]{0:T(1024)S(1)}, u32[]{:S(2)}, u32[]{:S(2)}) collective-permute-start(f32[2048]{0:T(1024)S(1)} %add_add_fusion.10), channel_id=1, source_target_pairs={{0,1},{1,0},{2,3},{3,2},{4,5},{5,4},{6,7},{7,6},{8,9},{9,8},{10,11... | collective-permute-start | bytes 24584 | tf_op jit(solution)/shard_map/ppermute | solution.py:47
  202.1 19.2 %collective-permute-start.39 = (f32[8,128,128]{2,1,0:T(8,128)}, f32[8,128,128]{2,1,0:T(8,128)}, u32[]{:S(2)}, u32[]{:S(2)}) collective-permute-start(f32[8,128,128]{2,1,0:T(8,128)} %get-tuple-element.11), channel_id=1, source_target_pairs={{16,0},{32,16},{48,32},{64,48},{80,64},{96,80},{112,96},{128,112},... | collective-permute-start | bytes 1572872 | tf_op jit(solution)/shard_map/ppermute | solution.py:31
  206.5 14.8 %collective-permute-start.38 = (f32[8,128,128]{2,1,0:T(8,128)}, f32[8,128,128]{2,1,0:T(8,128)}, u32[]{:S(2)}, u32[]{:S(2)}) collective-permute-start(f32[8,128,128]{2,1,0:T(8,128)} %get-tuple-element.10), channel_id=1, source_target_pairs={{0,16},{16,32},{32,48},{48,64},{64,80},{80,96},{96,112},{112,128},... | collective-permute-start | bytes 1572872 | tf_op jit(solution)/shard_map/ppermute | solution.py:31
  230.3 10.5 %collective-permute-start.55 = (f32[]{:T(128)}, f32[]{:T(128)}, u32[]{:S(2)}, u32[]{:S(2)}) collective-permute-start(f32[]{:T(128)} %add.572), channel_id=1, source_target_pairs={{0,64},{16,80},{32,96},{48,112},{64,0},{80,16},{96,32},{112,48},{1... | collective-permute-start | bytes 20 | tf_op jit(solution)/shard_map/ppermute | solution.py:47
  294.9 10.5 %collective-permute-start.71 = (f32[]{:T(128)}, f32[]{:T(128)}, u32[]{:S(2)}, u32[]{:S(2)}) collective-permute-start(f32[]{:T(128)} %add.590), channel_id=1, source_target_pairs={{0,64},{16,80},{32,96},{48,112},{64,0},{80,16},{96,32},{112,48},{1... | collective-permute-start | bytes 20 | tf_op jit(solution)/shard_map/ppermute | solution.py:47
  348.2 19.6 %collective-permute-start.81 = (f32[8,128,128]{2,1,0:T(8,128)S(1)}, f32[8,128,128]{2,1,0:T(8,128)S(1)}, u32[]{:S(2)}, u32[]{:S(2)}) collective-permute-start(f32[8,128,128]{2,1,0:T(8,128)S(1)} %get-tuple-element.23), channel_id=1, source_target_pairs={{16,0},{32,16},{48,32},{64,48},{80,64},{96,80},{112,96},{128,112},... | collective-permute-start | bytes 1572872 | tf_op jit(solution)/shard_map/ppermute | solution.py:23
  350.9 16.9 %collective-permute-start.80 = (f32[8,128,128]{2,1,0:T(8,128)S(1)}, f32[8,128,128]{2,1,0:T(8,128)S(1)}, u32[]{:S(2)}, u32[]{:S(2)}) collective-permute-start(f32[8,128,128]{2,1,0:T(8,128)S(1)} %get-tuple-element.22), channel_id=1, source_target_pairs={{0,16},{16,32},{32,48},{48,64},{64,80},{80,96},{96,112},{112,128},... | collective-permute-start | bytes 1572872 | tf_op jit(solution)/shard_map/ppermute | solution.py:20
  364.1 30.1 %collective-permute-start.91 = (f32[2048]{0:T(1024)S(1)}, f32[2048]{0:T(1024)S(1)}, u32[]{:S(2)}, u32[]{:S(2)}) collective-permute-start(f32[2048]{0:T(1024)S(1)} %add_add_fusion.6), channel_id=1, source_target_pairs={{0,2},{1,3},{2,0},{3,1},{4,6},{5,7},{6,4},{7,5},{8,10},{9,11},{10,... | collective-permute-start | bytes 24584 | tf_op jit(solution)/shard_map/ppermute | solution.py:47
  364.1 30.1 %collective-permute-start.92 = (f32[2048]{0:T(1024)S(1)}, f32[2048]{0:T(1024)S(1)}, u32[]{:S(2)}, u32[]{:S(2)}) collective-permute-start(f32[2048]{0:T(1024)S(1)} %add_add_fusion.6), channel_id=1, source_target_pairs={{0,3},{1,2},{2,1},{3,0},{4,7},{5,6},{6,5},{7,4},{8,11},{9,10},{10,... | collective-permute-start | bytes 24584 | tf_op jit(solution)/shard_map/ppermute | solution.py:47
  365.0 29.2 %collective-permute-start.90 = (f32[2048]{0:T(1024)S(1)}, f32[2048]{0:T(1024)S(1)}, u32[]{:S(2)}, u32[]{:S(2)}) collective-permute-start(f32[2048]{0:T(1024)S(1)} %add_add_fusion.6), channel_id=1, source_target_pairs={{0,1},{1,0},{2,3},{3,2},{4,5},{5,4},{6,7},{7,6},{8,9},{9,8},{10,11... | collective-permute-start | bytes 24584 | tf_op jit(solution)/shard_map/ppermute | solution.py:47
  389.8 18.1 %collective-permute-start.83 = (f32[8,128,128]{2,1,0:T(8,128)}, f32[8,128,128]{2,1,0:T(8,128)}, u32[]{:S(2)}, u32[]{:S(2)}) collective-permute-start(f32[8,128,128]{2,1,0:T(8,128)} %get-tuple-element.9), channel_id=1, source_target_pairs={{16,0},{32,16},{48,32},{64,48},{80,64},{96,80},{112,96},{128,112},... | collective-permute-start | bytes 1572872 | tf_op jit(solution)/shard_map/ppermute | solution.py:31
  391.7 16.2 %collective-permute-start.82 = (f32[8,128,128]{2,1,0:T(8,128)}, f32[8,128,128]{2,1,0:T(8,128)}, u32[]{:S(2)}, u32[]{:S(2)}) collective-permute-start(f32[8,128,128]{2,1,0:T(8,128)} %get-tuple-element.8), channel_id=1, source_target_pairs={{0,16},{16,32},{32,48},{48,64},{64,80},{80,96},{96,112},{112,128},... | collective-permute-start | bytes 1572872 | tf_op jit(solution)/shard_map/ppermute | solution.py:31
  (103 other events, 681.2 us)

commit v2 on v1

--- a/solution.py
+++ b/solution.py
@@ -127,21 +127,23 @@
                 owned = owned + jnp.pad(arrived, ((block_x - W, 0), (0, 0), (0, 0)))
         return owned
 
-    def precondition(field):
-        coeffs = (
-            transform_cross(transform_first(widen(field), table_x), table_y, table_z) / spectrum
-        )
-        local_part = fold_back(transform_cross(transform_first(coeffs, table_x), table_y, table_z))
+    slot = lax.axis_index("wide") * lax.axis_size("narrow") + lax.axis_index("narrow")
+
+    def placed_means(field):
         octant_means = (
             field.reshape(2, block_x // 2, 2, block_y // 2, 2, block_z // 2)
             .mean(axis=(1, 3, 5))
             .reshape(PRIMAL)
         )
-        slot = lax.axis_index("wide") * lax.axis_size("narrow") + lax.axis_index("narrow")
-        placed = lax.dynamic_update_slice(
+        return lax.dynamic_update_slice(
             jnp.zeros((coarse_rows.shape[1],), octant_means.dtype), octant_means, (slot * PRIMAL,)
         )
-        all_means = total_over(placed)
+
+    def precondition(field, all_means):
+        coeffs = (
+            transform_cross(transform_first(widen(field), table_x), table_y, table_z) / spectrum
+        )
+        local_part = fold_back(transform_cross(transform_first(coeffs, table_x), table_y, table_z))
         correction = jnp.dot(coarse_rows, all_means, precision=lax.Precision.HIGHEST).reshape(
             2, 2, 2
         )
@@ -151,31 +153,60 @@
         )
         return local_part + spread.reshape(block_x, block_y, block_z)
 
-    def inner_norm(residual, preconditioned):
-        return total_over(jnp.sum(residual * preconditioned))
-
-    solution = jnp.zeros_like(source)
+    def apply_matrix(field):
+        padded_field = with_halo(field, (("wide", 0), ("narrow", 1)), 1)
+        return operate(field, padded_field, reaction, face_x, face_y, face_z)
+
     residual = source
-    preconditioned = precondition(residual)
-    direction = preconditioned
-    gamma_now = None
-    for iteration in range(ITERS):
-        padded_field = with_halo(direction, (("wide", 0), ("narrow", 1)), 1)
-        image = operate(direction, padded_field, reaction, face_x, face_y, face_z)
-        if gamma_now is None:
-            both = total_over(
-                jnp.stack([jnp.sum(residual * preconditioned), jnp.sum(direction * image)])
+    residual_means = total_over(placed_means(residual))
+    preconditioned = precondition(residual, residual_means)
+    bent = apply_matrix(preconditioned)
+    sums = total_over(
+        jnp.concatenate(
+            [
+                jnp.stack([jnp.sum(residual * preconditioned), jnp.sum(preconditioned * bent)]),
+                placed_means(bent),
+            ]
+        )
+    )
+    gamma_now, curvature, image_means = sums[0], sums[1], sums[2:]
+    direction, image = preconditioned, bent
+    step_size = gamma_now / curvature
+    solution = step_size * direction
+    residual = residual - step_size * image
+    residual_means = residual_means - step_size * image_means
+    for iteration in range(1, ITERS):
+        preconditioned = precondition(residual, residual_means)
+        bent = apply_matrix(preconditioned)
+        sums = total_over(
+            jnp.concatenate(
+                [
+                    jnp.stack(
+                        [
+                            jnp.sum(residual * preconditioned),
+                            jnp.sum(preconditioned * bent),
+                            jnp.sum(preconditioned * image),
+                            jnp.sum(direction * bent),
+                        ]
+                    ),
+                    placed_means(bent),
+                ]
             )
-            gamma_now, curvature = both[0], both[1]
-        else:
-            curvature = total_over(jnp.sum(direction * image))
+        )
+        gamma_next = sums[0]
+        ratio = gamma_next / gamma_now
+        curvature = sums[1] + ratio * (sums[2] + sums[3]) + ratio * ratio * curvature
+        direction = preconditioned + ratio * direction
+        image = bent + ratio * image
+        image_means = sums[4:] + ratio * image_means
+        gamma_now = gamma_next
         step_size = gamma_now / curvature
         solution = solution + step_size * direction
         residual = residual - step_size * image
-        preconditioned = precondition(residual)
-        gamma_next = inner_norm(residual, preconditioned)
-        direction = preconditioned + gamma_next / gamma_now * direction
-        gamma_now = gamma_next
+        residual_means = residual_means - step_size * image_means
+    preconditioned = precondition(residual, residual_means)
+    gamma_next = total_over(jnp.sum(residual * preconditioned))
+    direction = preconditioned + gamma_next / gamma_now * direction
     return (solution, residual, direction)
 
 

time: 468 us -> 379 us (0.81); the launches traced: 459 us -> 377 us
  starting transfers between devices: 219 us -> 143 us
  between operations: 29.6 us -> 16.6 us
  waiting for transfers between devices: 68.2 us -> 74.5 us
  other arithmetic: 38.4 us -> 32.2 us
  local copies, waits for them, and re-layouts: 32.1 us -> 37.3 us
    ppermute x84 -> x48, starting transfers between devices: 163 us -> 87.1 us  [total_over(): lax.ppermute(value, axis, [(i, i ^ j * stride) for i in range(count)])]
    ppermute x84 -> x48, waiting for transfers between devices: 52.7 us -> 41.7 us  [total_over(): lax.ppermute(value, axis, [(i, i ^ j * stride) for i in range(count)])]
    ppermute x9, waiting for transfers between devices: 6.27 us -> 13.9 us  [with_halo(): lax.ppermute(lax.slice_in_dim(block, block.shape[dim] - width, None, axis...]
    ppermute x9, waiting for transfers between devices: 7.25 us -> 14.8 us  [with_halo(): lax.ppermute(lax.slice_in_dim(block, 0, width, axis=dim), axis, backward)]
    reduce_sum x7 -> x6, other arithmetic: 20.2 us -> 17.8 us  [the longest x3 8.35 us: placed_means(): octant_means = field.reshape(2, block_x // 2, 2, block_y // 2, 2, block_z...]
  transfers between devices with their start and end apart: 108 -> 72, of which waited for: 45 -> 37; matrix products, arithmetic and copies ran while one was open for 15% -> 7% of each run, Pallas kernels for 0% -> 0%
where the time goes in v2:
time: 379 us; the launch traced here: 377 us
  starting transfers between devices  143 us (38%)
  waiting for transfers between devices  74.5 us (20%)
  matrix products  73.2 us (19%)
  local copies, waits for them, and re-layouts  37.3 us (10%)
  other arithmetic  32.2 us (8%)
  between operations  16.6 us (4%)
    ppermute x48, starting transfers between devices, total_over(): lax.ppermute(value, axis, [(i, i ^ j * stride) for i in range(count)])  87.1 us
    ppermute x48, waiting for transfers between devices, total_over(): lax.ppermute(value, axis, [(i, i ^ j * stride) for i in range(count)])  41.7 us
    dot_general x6, matrix products, transform_first(): jnp.einsum('ryz,re->eyz', field, table_x, precision=lax.Precision.HIGHEST)  32.4 us
    ppermute x9, starting transfers between devices, with_halo(): lax.ppermute(lax.slice_in_dim(block, block.shape[dim] - width, None, axis...  23.1 us
    dot_general x6, matrix products, transform_cross(): jnp.einsum('ryz,zc->ryc', field, table_z, precision=lax.Precision.HIGHEST)  22 us
    ppermute x9, starting transfers between devices, with_halo(): lax.ppermute(lax.slice_in_dim(block, 0, width, axis=dim), axis, backward)  19.6 us
    ppermute x9, waiting for transfers between devices, with_halo(): lax.ppermute(lax.slice_in_dim(block, 0, width, axis=dim), axis, backward)  14.8 us
    ppermute x9, waiting for transfers between devices, with_halo(): lax.ppermute(lax.slice_in_dim(block, block.shape[dim] - width, None, axis...  13.9 us
  transfers between devices with their start and end apart: 72, of which 37 were waited for; matrix products, arithmetic and copies ran while one was open for 7% of the time, Pallas kernels for 0%

profile of v2, /device:TPU:32, one launch (start us, length us, event | category | flops | bytes accessed | tf_op | source)
XLA Modules:
  0.0 376.7 jit_solution(1455241251056493713)
XLA Ops:
  9.3 3.6 collective-permute-start.1
  15.4 5.5 %collective-permute-start.8 = (f32[2048]{0:T(1024)S(1)}, f32[2048]{0:T(1024)S(1)}, u32[]{:S(2)}, u32[]{:S(2)}) collective-permute-start(f32[2048]{0:T(1024)S(1)} %add_add_fusion.15), channel_id=1, source_target_pairs={{0,128},{16,144},{32,160},{48,176},{64,192},{80,208},{96,224},{112... | collective-permute-start | bytes 24584 | tf_op jit(solution)/shard_map/ppermute | solution.py:47
  43.0 3.6 collective-permute-start.17
  59.3 3.7 fusion.20
  65.2 16.3 %fusion.2 = f32[32,128,128]{2,0,1:T(8,128)S(1)} fusion(f32[128,32,128]{2,0,1:T(8,128)S(1)} %fusion.81, f32[128]{0:T(128)S(1)} %copy-done.23, f32[32,128]{0,1:T(8,128)S(1)} %broadcast_add_fusion, f32[32]{0:T(128)S(1)} %copy-done.20, f32[32]{0:T(128)S(1)} %copy-done.21), kind=kOutput, calls=%fused_computation.8 | convolution fusion | flops 202902528 | bytes 4211456 | tf_op jit(solution)/shard_map/ryz,re->eyz/dot_general | solution.py:95
  81.5 3.7 fusion.17
  93.3 4.5 %collective-permute-start.20 = (f32[18,1,128]{2,1,0:T(1,128)S(1)}, f32[18,1,128]{2,1,0:T(1,128)S(1)}, u32[]{:S(2)}, u32[]{:S(2)}) collective-permute-start(f32[18,1,128]{2,1,0:T(1,128)S(1)} %get-tuple-element.23), channel_id=1, source_target_pairs={{0,1},{1,2},{2,3},{3,4},{4,5},{5,6},{6,7},{7,8},{8,9},{9,10},{10,1... | collective-permute-start | bytes 27656 | tf_op jit(solution)/shard_map/ppermute | solution.py:20
  111.5 3.6 collective-permute-done.22
  129.9 7.9 %collective-permute-start.28 = (f32[2050]{0:T(1024)S(1)}, f32[2050]{0:T(1024)S(1)}, u32[]{:S(2)}, u32[]{:S(2)}) collective-permute-start(f32[2050]{0:T(1024)S(1)} %add_add_fusion.11), channel_id=1, source_target_pairs={{0,128},{16,144},{32,160},{48,176},{64,192},{80,208},{96,224},{112... | collective-permute-start | bytes 24608 | tf_op jit(solution)/shard_map/ppermute | solution.py:47
  139.5 4.3 %collective-permute-done.29 = f32[2050]{0:T(1024)S(1)} collective-permute-done((f32[2050]{0:T(1024)S(1)}, f32[2050]{0:T(1024)S(1)}, u32[]{:S(2)}, u32[]{:S(2)}) %collective-permute-start.29) | collective-permute-done | bytes 8232 | tf_op jit(solution)/shard_map/ppermute | solution.py:47
  143.7 4.5 %collective-permute-start.31 = (f32[2050]{0:T(1024)S(1)}, f32[2050]{0:T(1024)S(1)}, u32[]{:S(2)}, u32[]{:S(2)}) collective-permute-start(f32[2050]{0:T(1024)S(1)} %add_add_fusion.10), channel_id=1, source_target_pairs={{0,2},{1,3},{2,0},{3,1},{4,6},{5,7},{6,4},{7,5},{8,10},{9,11},{10,... | collective-permute-start | bytes 24608 | tf_op jit(solution)/shard_map/ppermute | solution.py:47
  170.1 3.9 %collective-permute-done.37 = f32[8,128,128]{2,1,0:T(8,128)S(1)} collective-permute-done((f32[8,128,128]{2,1,0:T(8,128)S(1)}, f32[8,128,128]{2,1,0:T(8,128)S(1)}, u32[]{:S(2)}, u32[]{:S(2)}) %collective-permute-start.37) | collective-permute-done | bytes 524320 | tf_op jit(solution)/shard_map/ppermute | solution.py:23
  173.9 3.8 %collective-permute-done.36 = f32[8,128,128]{2,1,0:T(8,128)S(1)} collective-permute-done((f32[8,128,128]{2,1,0:T(8,128)S(1)}, f32[8,128,128]{2,1,0:T(8,128)S(1)}, u32[]{:S(2)}, u32[]{:S(2)}) %collective-permute-start.36) | collective-permute-done | bytes 524320 | tf_op jit(solution)/shard_map/ppermute | solution.py:20
  181.1 3.7 fusion.13
  190.4 3.7 fusion.10
  244.9 5.8 %collective-permute-start.48 = (f32[2052]{0:T(1024)S(1)}, f32[2052]{0:T(1024)S(1)}, u32[]{:S(2)}, u32[]{:S(2)}) collective-permute-start(f32[2052]{0:T(1024)S(1)} %add_add_fusion.7), channel_id=1, source_target_pairs={{0,128},{16,144},{32,160},{48,176},{64,192},{80,208},{96,224},{112... | collective-permute-start | bytes 24632 | tf_op jit(solution)/shard_map/ppermute | solution.py:47
  252.6 4.1 %collective-permute-done.49 = f32[2052]{0:T(1024)S(1)} collective-permute-done((f32[2052]{0:T(1024)S(1)}, f32[2052]{0:T(1024)S(1)}, u32[]{:S(2)}, u32[]{:S(2)}) %collective-permute-start.49) | collective-permute-done | bytes 8240 | tf_op jit(solution)/shard_map/ppermute | solution.py:47
  284.3 3.9 %collective-permute-done.57 = f32[8,128,128]{2,1,0:T(8,128)S(1)} collective-permute-done((f32[8,128,128]{2,1,0:T(8,128)S(1)}, f32[8,128,128]{2,1,0:T(8,128)S(1)}, u32[]{:S(2)}, u32[]{:S(2)}) %collective-permute-start.57) | collective-permute-done | bytes 524320 | tf_op jit(solution)/shard_map/ppermute | solution.py:23
  288.1 3.8 %collective-permute-done.56 = f32[8,128,128]{2,1,0:T(8,128)S(1)} collective-permute-done((f32[8,128,128]{2,1,0:T(8,128)S(1)}, f32[8,128,128]{2,1,0:T(8,128)S(1)}, u32[]{:S(2)}, u32[]{:S(2)}) %collective-permute-start.56) | collective-permute-done | bytes 524320 | tf_op jit(solution)/shard_map/ppermute | solution.py:20
  295.3 3.7 fusion.6
  304.6 3.7 fusion.3
  336.7 4.6 %collective-permute-start.64 = (f32[]{:T(128)}, f32[]{:T(128)}, u32[]{:S(2)}, u32[]{:S(2)}) collective-permute-start(f32[]{:T(128)} %add.494), channel_id=1, source_target_pairs={{0,128},{16,144},{32,160},{48,176},{64,192},{80,208},{96,224},{112... | collective-permute-start | bytes 20 | tf_op jit(solution)/shard_map/ppermute | solution.py:47
  361.4 4.8 %collective-permute-start.70 = (f32[]{:T(128)}, f32[]{:T(128)}, u32[]{:S(2)}, u32[]{:S(2)}) collective-permute-start(f32[]{:T(128)} %add.500), channel_id=1, source_target_pairs={{0,8},{1,9},{2,10},{3,11},{4,12},{5,13},{6,14},{7,15},{8,0},{9,1},... | collective-permute-start | bytes 20 | tf_op jit(solution)/shard_map/ppermute | solution.py:47
  372.8 3.7 multiply_add_fusion
  (269 shorter events, 245.9 us)
Async XLA Ops:
  7.3 8.0 %collective-permute-start.5 = (f32[2048]{0:T(1024)S(1)}, f32[2048]{0:T(1024)S(1)}, u32[]{:S(2)}, u32[]{:S(2)}) collective-permute-start(f32[2048]{0:T(1024)S(1)} %dynamic_update_slice.11), channel_id=1, source_target_pairs={{0,32},{16,48},{32,0},{48,16},{64,96},{80,112},{96,64},{112,80},{1... | collective-permute-start | bytes 24584 | tf_op jit(solution)/shard_map/ppermute | solution.py:47
  9.3 45.5 %collective-permute-start.1 = (f32[8,128,128]{2,1,0:T(8,128)S(1)}, f32[8,128,128]{2,1,0:T(8,128)}, u32[]{:S(2)}, u32[]{:S(2)}) collective-permute-start(f32[8,128,128]{2,1,0:T(8,128)S(1)} %get-tuple-element.39), channel_id=1, source_target_pairs={{16,0},{32,16},{48,32},{64,48},{80,64},{96,80},{112,96},{128,112},... | collective-permute-start | bytes 1572872 | tf_op jit(solution)/shard_map/ppermute | solution.py:23
  13.0 41.9 %collective-permute-start = (f32[8,128,128]{2,1,0:T(8,128)S(1)}, f32[8,128,128]{2,1,0:T(8,128)}, u32[]{:S(2)}, u32[]{:S(2)}) collective-permute-start(f32[8,128,128]{2,1,0:T(8,128)S(1)} %get-tuple-element.38), channel_id=1, source_target_pairs={{0,16},{16,32},{32,48},{48,64},{64,80},{80,96},{96,112},{112,128},... | collective-permute-start | bytes 1572872 | tf_op jit(solution)/shard_map/ppermute | solution.py:20
  15.4 10.4 %collective-permute-start.8 = (f32[2048]{0:T(1024)S(1)}, f32[2048]{0:T(1024)S(1)}, u32[]{:S(2)}, u32[]{:S(2)}) collective-permute-start(f32[2048]{0:T(1024)S(1)} %add_add_fusion.15), channel_id=1, source_target_pairs={{0,128},{16,144},{32,160},{48,176},{64,192},{80,208},{96,224},{112... | collective-permute-start | bytes 24584 | tf_op jit(solution)/shard_map/ppermute | solution.py:47
  40.7 13.7 %collective-permute-start.16 = (f32[1,128,128]{2,1,0:T(8,128)S(1)}, f32[1,128,128]{2,1,0:T(8,128)S(1)}, u32[]{:S(2)}, u32[]{:S(2)}) collective-permute-start(f32[1,128,128]{2,1,0:T(8,128)S(1)} %get-tuple-element.35), channel_id=1, source_target_pairs={{0,16},{16,32},{32,48},{48,64},{64,80},{80,96},{96,112},{112,128},... | collective-permute-start | bytes 196616 | tf_op jit(solution)/shard_map/ppermute | solution.py:20
  43.0 11.8 %collective-permute-start.17 = (f32[1,128,128]{2,1,0:T(8,128)S(1)}, f32[1,128,128]{2,1,0:T(8,128)S(1)}, u32[]{:S(2)}, u32[]{:S(2)}) collective-permute-start(f32[1,128,128]{2,1,0:T(8,128)S(1)} %get-tuple-element.34), channel_id=1, source_target_pairs={{16,0},{32,16},{48,32},{64,48},{80,64},{96,80},{112,96},{128,112},... | collective-permute-start | bytes 196616 | tf_op jit(solution)/shard_map/ppermute | solution.py:23
  87.5 10.6 %collective-permute-start.3 = (f32[8,128,128]{2,1,0:T(8,128)S(1)}, f32[8,128,128]{2,1,0:T(8,128)S(1)}, u32[]{:S(2)}, u32[]{:S(2)}) collective-permute-start(f32[8,128,128]{2,1,0:T(8,128)S(1)} %get-tuple-element.18), channel_id=1, source_target_pairs={{16,0},{32,16},{48,32},{64,48},{80,64},{96,80},{112,96},{128,112},... | collective-permute-start | bytes 1572872 | tf_op jit(solution)/shard_map/ppermute | solution.py:31
  89.6 10.5 %collective-permute-start.2 = (f32[8,128,128]{2,1,0:T(8,128)S(1)}, f32[8,128,128]{2,1,0:T(8,128)S(1)}, u32[]{:S(2)}, u32[]{:S(2)}) collective-permute-start(f32[8,128,128]{2,1,0:T(8,128)S(1)} %get-tuple-element.17), channel_id=1, source_target_pairs={{0,16},{16,32},{32,48},{48,64},{64,80},{80,96},{96,112},{112,128},... | collective-permute-start | bytes 1572872 | tf_op jit(solution)/shard_map/ppermute | solution.py:31
  92.0 12.6 %collective-permute-start.21 = (f32[18,1,128]{2,1,0:T(1,128)S(1)}, f32[18,1,128]{2,1,0:T(1,128)S(1)}, u32[]{:S(2)}, u32[]{:S(2)}) collective-permute-start(f32[18,1,128]{2,1,0:T(1,128)S(1)} %get-tuple-element.24), channel_id=1, source_target_pairs={{1,0},{2,1},{3,2},{4,3},{5,4},{6,5},{7,6},{8,7},{9,8},{10,9},{11,1... | collective-permute-start | bytes 27656 | tf_op jit(solution)/shard_map/ppermute | solution.py:23
  93.3 11.3 %collective-permute-start.20 = (f32[18,1,128]{2,1,0:T(1,128)S(1)}, f32[18,1,128]{2,1,0:T(1,128)S(1)}, u32[]{:S(2)}, u32[]{:S(2)}) collective-permute-start(f32[18,1,128]{2,1,0:T(1,128)S(1)} %get-tuple-element.23), channel_id=1, source_target_pairs={{0,1},{1,2},{2,3},{3,4},{4,5},{5,6},{6,7},{7,8},{8,9},{9,10},{10,1... | collective-permute-start | bytes 27656 | tf_op jit(solution)/shard_map/ppermute | solution.py:20
  129.9 9.6 %collective-permute-start.28 = (f32[2050]{0:T(1024)S(1)}, f32[2050]{0:T(1024)S(1)}, u32[]{:S(2)}, u32[]{:S(2)}) collective-permute-start(f32[2050]{0:T(1024)S(1)} %add_add_fusion.11), channel_id=1, source_target_pairs={{0,128},{16,144},{32,160},{48,176},{64,192},{80,208},{96,224},{112... | collective-permute-start | bytes 24608 | tf_op jit(solution)/shard_map/ppermute | solution.py:47
  165.3 8.6 %collective-permute-start.37 = (f32[8,128,128]{2,1,0:T(8,128)S(1)}, f32[8,128,128]{2,1,0:T(8,128)S(1)}, u32[]{:S(2)}, u32[]{:S(2)}) collective-permute-start(f32[8,128,128]{2,1,0:T(8,128)S(1)} %get-tuple-element.30), channel_id=1, source_target_pairs={{16,0},{32,16},{48,32},{64,48},{80,64},{96,80},{112,96},{128,112},... | collective-permute-start | bytes 1572872 | tf_op jit(solution)/shard_map/ppermute | solution.py:23
  167.2 10.5 %collective-permute-start.36 = (f32[8,128,128]{2,1,0:T(8,128)S(1)}, f32[8,128,128]{2,1,0:T(8,128)S(1)}, u32[]{:S(2)}, u32[]{:S(2)}) collective-permute-start(f32[8,128,128]{2,1,0:T(8,128)S(1)} %get-tuple-element.29), channel_id=1, source_target_pairs={{0,16},{16,32},{32,48},{48,64},{64,80},{80,96},{96,112},{112,128},... | collective-permute-start | bytes 1572872 | tf_op jit(solution)/shard_map/ppermute | solution.py:20
  197.7 11.6 %collective-permute-start.39 = (f32[8,128,128]{2,1,0:T(8,128)S(1)}, f32[8,128,128]{2,1,0:T(8,128)}, u32[]{:S(2)}, u32[]{:S(2)}) collective-permute-start(f32[8,128,128]{2,1,0:T(8,128)S(1)} %get-tuple-element.16), channel_id=1, source_target_pairs={{16,0},{32,16},{48,32},{64,48},{80,64},{96,80},{112,96},{128,112},... | collective-permute-start | bytes 1572872 | tf_op jit(solution)/shard_map/ppermute | solution.py:31
  199.6 10.6 %collective-permute-start.38 = (f32[8,128,128]{2,1,0:T(8,128)S(1)}, f32[8,128,128]{2,1,0:T(8,128)}, u32[]{:S(2)}, u32[]{:S(2)}) collective-permute-start(f32[8,128,128]{2,1,0:T(8,128)S(1)} %get-tuple-element.15), channel_id=1, source_target_pairs={{0,16},{16,32},{32,48},{48,64},{64,80},{80,96},{96,112},{112,128},... | collective-permute-start | bytes 1572872 | tf_op jit(solution)/shard_map/ppermute | solution.py:31
  279.5 8.6 %collective-permute-start.57 = (f32[8,128,128]{2,1,0:T(8,128)S(1)}, f32[8,128,128]{2,1,0:T(8,128)S(1)}, u32[]{:S(2)}, u32[]{:S(2)}) collective-permute-start(f32[8,128,128]{2,1,0:T(8,128)S(1)} %get-tuple-element.26), channel_id=1, source_target_pairs={{16,0},{32,16},{48,32},{64,48},{80,64},{96,80},{112,96},{128,112},... | collective-permute-start | bytes 1572872 | tf_op jit(solution)/shard_map/ppermute | solution.py:23
  281.5 10.5 %collective-permute-start.56 = (f32[8,128,128]{2,1,0:T(8,128)S(1)}, f32[8,128,128]{2,1,0:T(8,128)S(1)}, u32[]{:S(2)}, u32[]{:S(2)}) collective-permute-start(f32[8,128,128]{2,1,0:T(8,128)S(1)} %get-tuple-element.25), channel_id=1, source_target_pairs={{0,16},{16,32},{32,48},{48,64},{64,80},{80,96},{96,112},{112,128},... | collective-permute-start | bytes 1572872 | tf_op jit(solution)/shard_map/ppermute | solution.py:20
  312.9 11.6 %collective-permute-start.59 = (f32[8,128,128]{2,1,0:T(8,128)}, f32[8,128,128]{2,1,0:T(8,128)}, u32[]{:S(2)}, u32[]{:S(2)}) collective-permute-start(f32[8,128,128]{2,1,0:T(8,128)} %get-tuple-element.14), channel_id=1, source_target_pairs={{16,0},{32,16},{48,32},{64,48},{80,64},{96,80},{112,96},{128,112},... | collective-permute-start | bytes 1572872 | tf_op jit(solution)/shard_map/ppermute | solution.py:31
  314.8 10.8 %collective-permute-start.58 = (f32[8,128,128]{2,1,0:T(8,128)}, f32[8,128,128]{2,1,0:T(8,128)}, u32[]{:S(2)}, u32[]{:S(2)}) collective-permute-start(f32[8,128,128]{2,1,0:T(8,128)} %get-tuple-element.13), channel_id=1, source_target_pairs={{0,16},{16,32},{32,48},{48,64},{64,80},{80,96},{96,112},{112,128},... | collective-permute-start | bytes 1572872 | tf_op jit(solution)/shard_map/ppermute | solution.py:31
  333.4 10.7 %collective-permute-start.63 = (f32[]{:T(128)}, f32[]{:T(128)}, u32[]{:S(2)}, u32[]{:S(2)}) collective-permute-start(f32[]{:T(128)} %add.494), channel_id=1, source_target_pairs={{0,64},{16,80},{32,96},{48,112},{64,0},{80,16},{96,32},{112,48},{1... | collective-permute-start | bytes 20 | tf_op jit(solution)/shard_map/ppermute | solution.py:47
  336.7 8.2 %collective-permute-start.64 = (f32[]{:T(128)}, f32[]{:T(128)}, u32[]{:S(2)}, u32[]{:S(2)}) collective-permute-start(f32[]{:T(128)} %add.494), channel_id=1, source_target_pairs={{0,128},{16,144},{32,160},{48,176},{64,192},{80,208},{96,224},{112... | collective-permute-start | bytes 20 | tf_op jit(solution)/shard_map/ppermute | solution.py:47
  348.4 8.7 %collective-permute-start.66 = (f32[]{:T(128)}, f32[]{:T(128)}, u32[]{:S(2)}, u32[]{:S(2)}) collective-permute-start(f32[]{:T(128)} %add.497), channel_id=1, source_target_pairs={{0,1},{1,0},{2,3},{3,2},{4,5},{5,4},{6,7},{7,6},{8,9},{9,8},{10,11... | collective-permute-start | bytes 20 | tf_op jit(solution)/shard_map/ppermute | solution.py:47
  360.1 8.7 %collective-permute-start.69 = (f32[]{:T(128)}, f32[]{:T(128)}, u32[]{:S(2)}, u32[]{:S(2)}) collective-permute-start(f32[]{:T(128)} %add.500), channel_id=1, source_target_pairs={{0,4},{1,5},{2,6},{3,7},{4,0},{5,1},{6,2},{7,3},{8,12},{9,13},{10,... | collective-permute-start | bytes 20 | tf_op jit(solution)/shard_map/ppermute | solution.py:47
  361.4 8.0 %collective-permute-start.70 = (f32[]{:T(128)}, f32[]{:T(128)}, u32[]{:S(2)}, u32[]{:S(2)}) collective-permute-start(f32[]{:T(128)} %add.500), channel_id=1, source_target_pairs={{0,8},{1,9},{2,10},{3,11},{4,12},{5,13},{6,14},{7,15},{8,0},{9,1},... | collective-permute-start | bytes 20 | tf_op jit(solution)/shard_map/ppermute | solution.py:47
  (72 other events, 474.3 us)

commit v3 on v2

--- a/solution.py
+++ b/solution.py
@@ -130,11 +130,10 @@
     slot = lax.axis_index("wide") * lax.axis_size("narrow") + lax.axis_index("narrow")
 
     def placed_means(field):
-        octant_means = (
-            field.reshape(2, block_x // 2, 2, block_y // 2, 2, block_z // 2)
-            .mean(axis=(1, 3, 5))
-            .reshape(PRIMAL)
-        )
+        along_x = field.reshape(2, block_x // 2, block_y, block_z).sum(axis=1)
+        along_y = along_x.reshape(2, 2, block_y // 2, block_z).sum(axis=2)
+        along_z = along_y.reshape(2, 2, 2, block_z // 2).sum(axis=3)
+        octant_means = (along_z / ((block_x // 2) * (block_y // 2) * (block_z // 2))).reshape(PRIMAL)
         return lax.dynamic_update_slice(
             jnp.zeros((coarse_rows.shape[1],), octant_means.dtype), octant_means, (slot * PRIMAL,)
         )
@@ -147,9 +146,10 @@
         correction = jnp.dot(coarse_rows, all_means, precision=lax.Precision.HIGHEST).reshape(
             2, 2, 2
         )
+        upper_z = lax.broadcasted_iota(jnp.int32, (1, 1, block_z), 2) >= block_z // 2
+        rows = jnp.where(upper_z, correction[:, :, 1:2], correction[:, :, 0:1])
         spread = jnp.broadcast_to(
-            correction[:, None, :, None, :, None],
-            (2, block_x // 2, 2, block_y // 2, 2, block_z // 2),
+            rows[:, None, :, None, :], (2, block_x // 2, 2, block_y // 2, block_z)
         )
         return local_part + spread.reshape(block_x, block_y, block_z)
 

time: 379 us -> 367 us (0.968); the launches traced: 377 us -> 360 us
  local copies, waits for them, and re-layouts: 37.3 us -> 16.1 us
  starting transfers between devices: 143 us -> 157 us
  matrix products: 73.2 us -> 60.9 us
  waiting for transfers between devices: 74.5 us -> 80.8 us
  other arithmetic: 32.2 us -> 27.7 us
    reshape x6 -> x3, local copies, waits for them, and re-layouts: 20.2 us -> 0.25 us  [placed_means(): along_z = along_y.reshape(2, 2, 2, block_z // 2).sum(axis=3)]
    dot_general x6, matrix products: 32.4 us -> 19.6 us  [transform_first(): jnp.einsum('ryz,re->eyz', field, table_x, precision=lax.Precision.HIGHEST)]
    ppermute x9, waiting for transfers between devices: 14.8 us -> 3.53 us  [with_halo(): lax.ppermute(lax.slice_in_dim(block, 0, width, axis=dim), axis, backward)]
    ppermute x6, waiting for transfers between devices: 4.08 us -> 13.5 us  [passed_along(): return lax.ppermute(block, axis, route)]
    ppermute x9, starting transfers between devices: 19.6 us -> 27.2 us  [with_halo(): lax.ppermute(lax.slice_in_dim(block, 0, width, axis=dim), axis, backward)]
    ppermute x48, waiting for transfers between devices: 41.7 us -> 47 us  [total_over(): lax.ppermute(value, axis, [(i, i ^ j * stride) for i in range(count)])]
    broadcast_in_dim x3 -> x6, local copies, waits for them, and re-layouts: 5.9 us -> 1 us  [the longest x3 0.71 us: precondition(): rows = jnp.where(upper_z, correction[:, :, 1:2], correction[:, :, 0:1])]
    ppermute x6, starting transfers between devices: 13.1 us -> 17.8 us  [passed_along(): return lax.ppermute(block, axis, route)]
  transfers between devices with their start and end apart: 72 -> 72, of which waited for: 37 -> 36; matrix products, arithmetic and copies ran while one was open for 7% -> 4% of each run, Pallas kernels for 0% -> 0%
where the time goes in v3:
time: 367 us; the launch traced here: 360 us
  starting transfers between devices  157 us (43%)
  waiting for transfers between devices  80.8 us (22%)
  matrix products  60.9 us (17%)
  other arithmetic  27.7 us (8%)
  between operations  17 us (5%)
  local copies, waits for them, and re-layouts  16.1 us (4%)
    ppermute x48, starting transfers between devices, total_over(): lax.ppermute(value, axis, [(i, i ^ j * stride) for i in range(count)])  89.1 us
    ppermute x48, waiting for transfers between devices, total_over(): lax.ppermute(value, axis, [(i, i ^ j * stride) for i in range(count)])  47 us
    ppermute x9, starting transfers between devices, with_halo(): lax.ppermute(lax.slice_in_dim(block, 0, width, axis=dim), axis, backward)  27.2 us
    ppermute x9, starting transfers between devices, with_halo(): lax.ppermute(lax.slice_in_dim(block, block.shape[dim] - width, None, axis...  23.2 us
    dot_general x6, matrix products, transform_cross(): jnp.einsum('ryz,zc->ryc', field, table_z, precision=lax.Precision.HIGHEST)  22 us
    dot_general x6, matrix products, transform_first(): jnp.einsum('ryz,re->eyz', field, table_x, precision=lax.Precision.HIGHEST)  19.6 us
    ppermute x6, starting transfers between devices, passed_along(): return lax.ppermute(block, axis, route)  17.8 us
    ppermute x9, waiting for transfers between devices, with_halo(): lax.ppermute(lax.slice_in_dim(block, block.shape[dim] - width, None, axis...  16.8 us
  transfers between devices with their start and end apart: 72, of which 36 were waited for; matrix products, arithmetic and copies ran while one was open for 4% of the time, Pallas kernels for 0%

profile of v3, /device:TPU:32, one launch (start us, length us, event | category | flops | bytes accessed | tf_op | source)
XLA Modules:
  0.0 359.8 jit_solution(16626508113536029844)
XLA Ops:
  15.6 4.4 %collective-permute-start.8 = (f32[2048]{0:T(1024)S(1)}, f32[2048]{0:T(1024)S(1)}, u32[]{:S(2)}, u32[]{:S(2)}) collective-permute-start(f32[2048]{0:T(1024)S(1)} %add_add_fusion.15), channel_id=1, source_target_pairs={{0,128},{16,144},{32,160},{48,176},{64,192},{80,208},{96,224},{112... | collective-permute-start | bytes 24584 | tf_op jit(solution)/shard_map/ppermute | solution.py:47
  42.5 4.2 %collective-permute-start.17 = (f32[1,128,128]{2,1,0:T(8,128)S(1)}, f32[1,128,128]{2,1,0:T(8,128)S(1)}, u32[]{:S(2)}, u32[]{:S(2)}) collective-permute-start(f32[1,128,128]{2,1,0:T(8,128)S(1)} %get-tuple-element.36), channel_id=1, source_target_pairs={{16,0},{32,16},{48,32},{64,48},{80,64},{96,80},{112,96},{128,112},... | collective-permute-start | bytes 196616 | tf_op jit(solution)/shard_map/ppermute | solution.py:23
  57.1 3.7 %fusion.20 = f32[32,128,128]{2,1,0:T(8,128)S(1)} fusion(f32[32,128,128]{2,0,1:T(8,128)S(1)} %fusion.22, f32[128]{0:T(128)S(1)} %iota_add_fusion.1, f32[128]{0:T(128)S(1)} %broadcast_multiply_fusion.4), kind=kOutput, calls=%fused_computation.26 | convolution fusion | flops 805355520 | bytes 4195328 | tf_op jit(solution)/shard_map/ryz,zc->ryc/dot_general | solution.py:99
  66.5 3.7 %fusion.17 = f32[32,128,128]{2,1,0:T(8,128)S(1)} fusion(f32[32,128,128]{2,0,1:T(8,128)S(1)} %fusion.2, f32[128]{0:T(128)S(1)} %iota_add_fusion.1, f32[128]{0:T(128)S(1)} %broadcast_multiply_fusion.4), kind=kOutput, calls=%fused_computation.23 | convolution fusion | flops 805355520 | bytes 4195328 | tf_op jit(solution)/shard_map/ryz,zc->ryc/dot_general | solution.py:99
  85.1 3.8 %collective-permute-start.18 = (f32[1,128,128]{2,1,0:T(8,128)S(1)}, f32[1,128,128]{2,1,0:T(8,128)S(1)}, u32[]{:S(2)}, u32[]{:S(2)}) collective-permute-start(f32[1,128,128]{2,1,0:T(8,128)S(1)} %get-tuple-element.39), channel_id=1, source_target_pairs={{16,0},{32,16},{48,32},{64,48},{80,64},{96,80},{112,96},{128,112},... | collective-permute-start | bytes 196616 | tf_op jit(solution)/shard_map/ppermute | solution.py:23
  95.8 4.7 %collective-permute-start.23 = (f32[18,1,128]{2,1,0:T(1,128)S(1)}, f32[18,1,128]{2,1,0:T(1,128)S(1)}, u32[]{:S(2)}, u32[]{:S(2)}) collective-permute-start(f32[18,1,128]{2,1,0:T(1,128)S(1)} %get-tuple-element.24), channel_id=1, source_target_pairs={{0,1},{1,2},{2,3},{3,4},{4,5},{5,6},{6,7},{7,8},{8,9},{9,10},{10,1... | collective-permute-start | bytes 27656 | tf_op jit(solution)/shard_map/ppermute | solution.py:20
  114.4 4.5 %collective-permute-start.28 = (f32[2050]{0:T(1024)S(1)}, f32[2050]{0:T(1024)S(1)}, u32[]{:S(2)}, u32[]{:S(2)}) collective-permute-start(f32[2050]{0:T(1024)S(1)} %add_add_fusion.11), channel_id=1, source_target_pairs={{0,128},{16,144},{32,160},{48,176},{64,192},{80,208},{96,224},{112... | collective-permute-start | bytes 24608 | tf_op jit(solution)/shard_map/ppermute | solution.py:47
  147.9 4.0 %collective-permute-start.37 = (f32[8,128,128]{2,1,0:T(8,128)S(1)}, f32[8,128,128]{2,1,0:T(8,128)S(1)}, u32[]{:S(2)}, u32[]{:S(2)}) collective-permute-start(f32[8,128,128]{2,1,0:T(8,128)S(1)} %get-tuple-element.32), channel_id=1, source_target_pairs={{16,0},{32,16},{48,32},{64,48},{80,64},{96,80},{112,96},{128,112},... | collective-permute-start | bytes 1572872 | tf_op jit(solution)/shard_map/ppermute | solution.py:23
  152.0 4.4 %collective-permute-done.36 = f32[8,128,128]{2,1,0:T(8,128)S(1)} collective-permute-done((f32[8,128,128]{2,1,0:T(8,128)S(1)}, f32[8,128,128]{2,1,0:T(8,128)S(1)}, u32[]{:S(2)}, u32[]{:S(2)}) %collective-permute-start.36) | collective-permute-done | bytes 524320 | tf_op jit(solution)/shard_map/ppermute | solution.py:20
  161.6 3.7 %fusion.13 = f32[32,128,128]{2,1,0:T(8,128)S(1)} fusion(f32[32,128,128]{2,0,1:T(8,128)S(1)} %fusion.15, f32[128]{0:T(128)S(1)} %iota_add_fusion.1, f32[128]{0:T(128)S(1)} %broadcast_multiply_fusion.4), kind=kOutput, calls=%fused_computation.19 | convolution fusion | flops 805355520 | bytes 4195328 | tf_op jit(solution)/shard_map/ryz,zc->ryc/dot_general | solution.py:99
  170.9 3.7 %fusion.10 = f32[32,128,128]{2,1,0:T(8,128)S(1)} fusion(f32[32,128,128]{2,0,1:T(8,128)S(1)} %fusion.1, f32[128]{0:T(128)S(1)} %iota_add_fusion.1, f32[128]{0:T(128)S(1)} %broadcast_multiply_fusion.4), kind=kOutput, calls=%fused_computation.16 | convolution fusion | flops 805355520 | bytes 4195328 | tf_op jit(solution)/shard_map/ryz,zc->ryc/dot_general | solution.py:99
  178.2 4.2 %collective-permute-start.38 = (f32[8,128,128]{2,1,0:T(8,128)S(1)}, f32[8,128,128]{2,1,0:T(8,128)}, u32[]{:S(2)}, u32[]{:S(2)}) collective-permute-start(f32[8,128,128]{2,1,0:T(8,128)S(1)} %get-tuple-element.17), channel_id=1, source_target_pairs={{0,16},{16,32},{32,48},{48,64},{64,80},{80,96},{96,112},{112,128},... | collective-permute-start | bytes 1572872 | tf_op jit(solution)/shard_map/ppermute | solution.py:31
  192.9 3.9 %collective-permute-start.40 = (f32[1,128,128]{2,1,0:T(8,128)S(1)}, f32[1,128,128]{2,1,0:T(8,128)S(1)}, u32[]{:S(2)}, u32[]{:S(2)}) collective-permute-start(f32[1,128,128]{2,1,0:T(8,128)S(1)} %get-tuple-element.30), channel_id=1, source_target_pairs={{16,0},{32,16},{48,32},{64,48},{80,64},{96,80},{112,96},{128,112},... | collective-permute-start | bytes 196616 | tf_op jit(solution)/shard_map/ppermute | solution.py:23
  203.7 4.8 %collective-permute-start.43 = (f32[18,1,128]{2,1,0:T(1,128)S(1)}, f32[18,1,128]{2,1,0:T(1,128)S(1)}, u32[]{:S(2)}, u32[]{:S(2)}) collective-permute-start(f32[18,1,128]{2,1,0:T(1,128)S(1)} %get-tuple-element.22), channel_id=1, source_target_pairs={{0,1},{1,2},{2,3},{3,4},{4,5},{5,6},{6,7},{7,8},{8,9},{9,10},{10,1... | collective-permute-start | bytes 27656 | tf_op jit(solution)/shard_map/ppermute | solution.py:20
  224.5 4.5 %collective-permute-start.48 = (f32[2052]{0:T(1024)S(1)}, f32[2052]{0:T(1024)S(1)}, u32[]{:S(2)}, u32[]{:S(2)}) collective-permute-start(f32[2052]{0:T(1024)S(1)} %add_add_fusion.7), channel_id=1, source_target_pairs={{0,128},{16,144},{32,160},{48,176},{64,192},{80,208},{96,224},{112... | collective-permute-start | bytes 24632 | tf_op jit(solution)/shard_map/ppermute | solution.py:47
  237.1 4.5 %collective-permute-start.51 = (f32[2052]{0:T(1024)S(1)}, f32[2052]{0:T(1024)S(1)}, u32[]{:S(2)}, u32[]{:S(2)}) collective-permute-start(f32[2052]{0:T(1024)S(1)} %add_add_fusion.6), channel_id=1, source_target_pairs={{0,2},{1,3},{2,0},{3,1},{4,6},{5,7},{6,4},{7,5},{8,10},{9,11},{10,... | collective-permute-start | bytes 24632 | tf_op jit(solution)/shard_map/ppermute | solution.py:47
  262.6 4.0 %collective-permute-start.57 = (f32[8,128,128]{2,1,0:T(8,128)S(1)}, f32[8,128,128]{2,1,0:T(8,128)S(1)}, u32[]{:S(2)}, u32[]{:S(2)}) collective-permute-start(f32[8,128,128]{2,1,0:T(8,128)S(1)} %get-tuple-element.28), channel_id=1, source_target_pairs={{16,0},{32,16},{48,32},{64,48},{80,64},{96,80},{112,96},{128,112},... | collective-permute-start | bytes 1572872 | tf_op jit(solution)/shard_map/ppermute | solution.py:23
  266.7 4.4 %collective-permute-done.56 = f32[8,128,128]{2,1,0:T(8,128)S(1)} collective-permute-done((f32[8,128,128]{2,1,0:T(8,128)S(1)}, f32[8,128,128]{2,1,0:T(8,128)S(1)}, u32[]{:S(2)}, u32[]{:S(2)}) %collective-permute-start.56) | collective-permute-done | bytes 524320 | tf_op jit(solution)/shard_map/ppermute | solution.py:20
  285.6 3.7 %fusion.3 = f32[32,128,128]{2,1,0:T(8,128)S(1)} fusion(f32[32,128,128]{2,0,1:T(8,128)S(1)} %fusion, f32[128]{0:T(128)S(1)} %iota_add_fusion.1, f32[128]{0:T(128)S(1)} %broadcast_multiply_fusion.4), kind=kOutput, calls=%fused_computation.9 | convolution fusion | flops 805355520 | bytes 4195328 | tf_op jit(solution)/shard_map/ryz,zc->ryc/dot_general | solution.py:99
  293.9 4.2 %collective-permute-start.58 = (f32[8,128,128]{2,1,0:T(8,128)}, f32[8,128,128]{2,1,0:T(8,128)}, u32[]{:S(2)}, u32[]{:S(2)}) collective-permute-start(f32[8,128,128]{2,1,0:T(8,128)} %get-tuple-element.15), channel_id=1, source_target_pairs={{0,16},{16,32},{32,48},{48,64},{64,80},{80,96},{96,112},{112,128},... | collective-permute-start | bytes 1572872 | tf_op jit(solution)/shard_map/ppermute | solution.py:31
  317.2 3.7 %collective-permute-start.64 = (f32[]{:T(128)}, f32[]{:T(128)}, u32[]{:S(2)}, u32[]{:S(2)}) collective-permute-start(f32[]{:T(128)} %add.494), channel_id=1, source_target_pairs={{0,128},{16,144},{32,160},{48,176},{64,192},{80,208},{96,224},{112... | collective-permute-start | bytes 20 | tf_op jit(solution)/shard_map/ppermute | solution.py:47
  320.8 5.1 %collective-permute-start.65 = (f32[]{:T(128)}, f32[]{:T(128)}, u32[]{:S(2)}, u32[]{:S(2)}) collective-permute-start(f32[]{:T(128)} %add.494), channel_id=1, source_target_pairs={{0,192},{16,208},{32,224},{48,240},{64,128},{80,144},{96,160},{112... | collective-permute-start | bytes 20 | tf_op jit(solution)/shard_map/ppermute | solution.py:47
  334.7 4.0 %collective-permute-start.68 = (f32[]{:T(128)}, f32[]{:T(128)}, u32[]{:S(2)}, u32[]{:S(2)}) collective-permute-start(f32[]{:T(128)} %add.497), channel_id=1, source_target_pairs={{0,3},{1,2},{2,1},{3,0},{4,7},{5,6},{6,5},{7,4},{8,11},{9,10},{10,... | collective-permute-start | bytes 20 | tf_op jit(solution)/shard_map/ppermute | solution.py:47
  355.9 3.7 %multiply_add_fusion = (f32[16,128,128]{2,1,0:T(8,128)}, f32[16,128,128]{2,1,0:T(8,128)}) fusion(f32[]{:T(128)S(6)} %div.129, f32[16,128,128]{2,1,0:T(8,128)S(1)} %fusion.42, f32[16,128,128]{2,1,0:T(8,128)S(1)} %fusion.59, f32[]{:T(128)S(6)} %div.126, f32[16,128,128]{2,1,0:T(8,128)} %bitcast.118, f32[8,128,128]{2,1,0:T(8,128)} %collective-permute-done.59, ...), kind=kLoop, calls=%fused_computation.98 | loop fusion | flops 2621440 | bytes 7340048 | tf_op jit(solution)/shard_map/add | solution.py:209
  (282 shorter events, 243.4 us)
Async XLA Ops:
  2.5 9.6 %collective-permute-start.4 = (f32[2048]{0:T(1024)S(1)}, f32[2048]{0:T(1024)S(1)}, u32[]{:S(2)}, u32[]{:S(2)}) collective-permute-start(f32[2048]{0:T(1024)S(1)} %dynamic_update_slice.11), channel_id=1, source_target_pairs={{0,16},{16,0},{32,48},{48,32},{64,80},{80,64},{96,112},{112,96},{1... | collective-permute-start | bytes 24584 | tf_op jit(solution)/shard_map/ppermute | solution.py:47
  2.6 9.7 %collective-permute-start.5 = (f32[2048]{0:T(1024)S(1)}, f32[2048]{0:T(1024)S(1)}, u32[]{:S(2)}, u32[]{:S(2)}) collective-permute-start(f32[2048]{0:T(1024)S(1)} %dynamic_update_slice.11), channel_id=1, source_target_pairs={{0,32},{16,48},{32,0},{48,16},{64,96},{80,112},{96,64},{112,80},{1... | collective-permute-start | bytes 24584 | tf_op jit(solution)/shard_map/ppermute | solution.py:47
  5.8 47.2 %collective-permute-start = (f32[8,128,128]{2,1,0:T(8,128)S(1)}, f32[8,128,128]{2,1,0:T(8,128)S(1)}, u32[]{:S(2)}, u32[]{:S(2)}) collective-permute-start(f32[8,128,128]{2,1,0:T(8,128)S(1)} %get-tuple-element.40), channel_id=1, source_target_pairs={{0,16},{16,32},{32,48},{48,64},{64,80},{80,96},{96,112},{112,128},... | collective-permute-start | bytes 1572872 | tf_op jit(solution)/shard_map/ppermute | solution.py:20
  8.0 45.0 %collective-permute-start.1 = (f32[8,128,128]{2,1,0:T(8,128)S(1)}, f32[8,128,128]{2,1,0:T(8,128)S(1)}, u32[]{:S(2)}, u32[]{:S(2)}) collective-permute-start(f32[8,128,128]{2,1,0:T(8,128)S(1)} %get-tuple-element.41), channel_id=1, source_target_pairs={{16,0},{32,16},{48,32},{64,48},{80,64},{96,80},{112,96},{128,112},... | collective-permute-start | bytes 1572872 | tf_op jit(solution)/shard_map/ppermute | solution.py:23
  12.3 9.7 %collective-permute-start.7 = (f32[2048]{0:T(1024)S(1)}, f32[2048]{0:T(1024)S(1)}, u32[]{:S(2)}, u32[]{:S(2)}) collective-permute-start(f32[2048]{0:T(1024)S(1)} %add_add_fusion.15), channel_id=1, source_target_pairs={{0,64},{16,80},{32,96},{48,112},{64,0},{80,16},{96,32},{112,48},{1... | collective-permute-start | bytes 24584 | tf_op jit(solution)/shard_map/ppermute | solution.py:47
  15.6 9.6 %collective-permute-start.8 = (f32[2048]{0:T(1024)S(1)}, f32[2048]{0:T(1024)S(1)}, u32[]{:S(2)}, u32[]{:S(2)}) collective-permute-start(f32[2048]{0:T(1024)S(1)} %add_add_fusion.15), channel_id=1, source_target_pairs={{0,128},{16,144},{32,160},{48,176},{64,192},{80,208},{96,224},{112... | collective-permute-start | bytes 24584 | tf_op jit(solution)/shard_map/ppermute | solution.py:47
  40.5 12.0 %collective-permute-start.16 = (f32[1,128,128]{2,1,0:T(8,128)S(1)}, f32[1,128,128]{2,1,0:T(8,128)S(1)}, u32[]{:S(2)}, u32[]{:S(2)}) collective-permute-start(f32[1,128,128]{2,1,0:T(8,128)S(1)} %get-tuple-element.37), channel_id=1, source_target_pairs={{0,16},{16,32},{32,48},{48,64},{64,80},{80,96},{96,112},{112,128},... | collective-permute-start | bytes 196616 | tf_op jit(solution)/shard_map/ppermute | solution.py:20
  42.5 10.5 %collective-permute-start.17 = (f32[1,128,128]{2,1,0:T(8,128)S(1)}, f32[1,128,128]{2,1,0:T(8,128)S(1)}, u32[]{:S(2)}, u32[]{:S(2)}) collective-permute-start(f32[1,128,128]{2,1,0:T(8,128)S(1)} %get-tuple-element.36), channel_id=1, source_target_pairs={{16,0},{32,16},{48,32},{64,48},{80,64},{96,80},{112,96},{128,112},... | collective-permute-start | bytes 196616 | tf_op jit(solution)/shard_map/ppermute | solution.py:23
  72.5 10.5 %collective-permute-start.2 = (f32[8,128,128]{2,1,0:T(8,128)S(1)}, f32[8,128,128]{2,1,0:T(8,128)S(1)}, u32[]{:S(2)}, u32[]{:S(2)}) collective-permute-start(f32[8,128,128]{2,1,0:T(8,128)S(1)} %get-tuple-element.19), channel_id=1, source_target_pairs={{0,16},{16,32},{32,48},{48,64},{64,80},{80,96},{96,112},{112,128},... | collective-permute-start | bytes 1572872 | tf_op jit(solution)/shard_map/ppermute | solution.py:31
  75.0 9.7 %collective-permute-start.3 = (f32[8,128,128]{2,1,0:T(8,128)S(1)}, f32[8,128,128]{2,1,0:T(8,128)S(1)}, u32[]{:S(2)}, u32[]{:S(2)}) collective-permute-start(f32[8,128,128]{2,1,0:T(8,128)S(1)} %get-tuple-element.20), channel_id=1, source_target_pairs={{16,0},{32,16},{48,32},{64,48},{80,64},{96,80},{112,96},{128,112},... | collective-permute-start | bytes 1572872 | tf_op jit(solution)/shard_map/ppermute | solution.py:31
  78.1 13.3 %collective-permute-start.20 = (f32[18,1,128]{2,1,0:T(1,128)S(1)}, f32[18,1,128]{2,1,0:T(1,128)S(1)}, u32[]{:S(2)}, u32[]{:S(2)}) collective-permute-start(f32[18,1,128]{2,1,0:T(1,128)S(1)} %get-tuple-element.25), channel_id=1, source_target_pairs={{0,1},{1,2},{2,3},{3,4},{4,5},{5,6},{6,7},{7,8},{8,9},{9,10},{10,1... | collective-permute-start | bytes 27656 | tf_op jit(solution)/shard_map/ppermute | solution.py:20
  79.4 12.0 %collective-permute-start.21 = (f32[18,1,128]{2,1,0:T(1,128)S(1)}, f32[18,1,128]{2,1,0:T(1,128)S(1)}, u32[]{:S(2)}, u32[]{:S(2)}) collective-permute-start(f32[18,1,128]{2,1,0:T(1,128)S(1)} %get-tuple-element.26), channel_id=1, source_target_pairs={{1,0},{2,1},{3,2},{4,3},{5,4},{6,5},{7,6},{8,7},{9,8},{10,9},{11,1... | collective-permute-start | bytes 27656 | tf_op jit(solution)/shard_map/ppermute | solution.py:23
  146.0 10.5 %collective-permute-start.36 = (f32[8,128,128]{2,1,0:T(8,128)S(1)}, f32[8,128,128]{2,1,0:T(8,128)S(1)}, u32[]{:S(2)}, u32[]{:S(2)}) collective-permute-start(f32[8,128,128]{2,1,0:T(8,128)S(1)} %get-tuple-element.31), channel_id=1, source_target_pairs={{0,16},{16,32},{32,48},{48,64},{64,80},{80,96},{96,112},{112,128},... | collective-permute-start | bytes 1572872 | tf_op jit(solution)/shard_map/ppermute | solution.py:20
  147.9 10.3 %collective-permute-start.37 = (f32[8,128,128]{2,1,0:T(8,128)S(1)}, f32[8,128,128]{2,1,0:T(8,128)S(1)}, u32[]{:S(2)}, u32[]{:S(2)}) collective-permute-start(f32[8,128,128]{2,1,0:T(8,128)S(1)} %get-tuple-element.32), channel_id=1, source_target_pairs={{16,0},{32,16},{48,32},{64,48},{80,64},{96,80},{112,96},{128,112},... | collective-permute-start | bytes 1572872 | tf_op jit(solution)/shard_map/ppermute | solution.py:23
  178.2 10.8 %collective-permute-start.38 = (f32[8,128,128]{2,1,0:T(8,128)S(1)}, f32[8,128,128]{2,1,0:T(8,128)}, u32[]{:S(2)}, u32[]{:S(2)}) collective-permute-start(f32[8,128,128]{2,1,0:T(8,128)S(1)} %get-tuple-element.17), channel_id=1, source_target_pairs={{0,16},{16,32},{32,48},{48,64},{64,80},{80,96},{96,112},{112,128},... | collective-permute-start | bytes 1572872 | tf_op jit(solution)/shard_map/ppermute | solution.py:31
  182.4 8.6 %collective-permute-start.39 = (f32[8,128,128]{2,1,0:T(8,128)S(1)}, f32[8,128,128]{2,1,0:T(8,128)}, u32[]{:S(2)}, u32[]{:S(2)}) collective-permute-start(f32[8,128,128]{2,1,0:T(8,128)S(1)} %get-tuple-element.18), channel_id=1, source_target_pairs={{16,0},{32,16},{48,32},{64,48},{80,64},{96,80},{112,96},{128,112},... | collective-permute-start | bytes 1572872 | tf_op jit(solution)/shard_map/ppermute | solution.py:31
  260.7 10.5 %collective-permute-start.56 = (f32[8,128,128]{2,1,0:T(8,128)S(1)}, f32[8,128,128]{2,1,0:T(8,128)S(1)}, u32[]{:S(2)}, u32[]{:S(2)}) collective-permute-start(f32[8,128,128]{2,1,0:T(8,128)S(1)} %get-tuple-element.27), channel_id=1, source_target_pairs={{0,16},{16,32},{32,48},{48,64},{64,80},{80,96},{96,112},{112,128},... | collective-permute-start | bytes 1572872 | tf_op jit(solution)/shard_map/ppermute | solution.py:20
  262.6 10.3 %collective-permute-start.57 = (f32[8,128,128]{2,1,0:T(8,128)S(1)}, f32[8,128,128]{2,1,0:T(8,128)S(1)}, u32[]{:S(2)}, u32[]{:S(2)}) collective-permute-start(f32[8,128,128]{2,1,0:T(8,128)S(1)} %get-tuple-element.28), channel_id=1, source_target_pairs={{16,0},{32,16},{48,32},{64,48},{80,64},{96,80},{112,96},{128,112},... | collective-permute-start | bytes 1572872 | tf_op jit(solution)/shard_map/ppermute | solution.py:23
  293.9 11.0 %collective-permute-start.58 = (f32[8,128,128]{2,1,0:T(8,128)}, f32[8,128,128]{2,1,0:T(8,128)}, u32[]{:S(2)}, u32[]{:S(2)}) collective-permute-start(f32[8,128,128]{2,1,0:T(8,128)} %get-tuple-element.15), channel_id=1, source_target_pairs={{0,16},{16,32},{32,48},{48,64},{64,80},{80,96},{96,112},{112,128},... | collective-permute-start | bytes 1572872 | tf_op jit(solution)/shard_map/ppermute | solution.py:31
  298.1 8.9 %collective-permute-start.59 = (f32[8,128,128]{2,1,0:T(8,128)}, f32[8,128,128]{2,1,0:T(8,128)}, u32[]{:S(2)}, u32[]{:S(2)}) collective-permute-start(f32[8,128,128]{2,1,0:T(8,128)} %get-tuple-element.16), channel_id=1, source_target_pairs={{16,0},{32,16},{48,32},{64,48},{80,64},{96,80},{112,96},{128,112},... | collective-permute-start | bytes 1572872 | tf_op jit(solution)/shard_map/ppermute | solution.py:31
  317.2 13.9 %collective-permute-start.64 = (f32[]{:T(128)}, f32[]{:T(128)}, u32[]{:S(2)}, u32[]{:S(2)}) collective-permute-start(f32[]{:T(128)} %add.494), channel_id=1, source_target_pairs={{0,128},{16,144},{32,160},{48,176},{64,192},{80,208},{96,224},{112... | collective-permute-start | bytes 20 | tf_op jit(solution)/shard_map/ppermute | solution.py:47
  320.8 10.3 %collective-permute-start.65 = (f32[]{:T(128)}, f32[]{:T(128)}, u32[]{:S(2)}, u32[]{:S(2)}) collective-permute-start(f32[]{:T(128)} %add.494), channel_id=1, source_target_pairs={{0,192},{16,208},{32,224},{48,240},{64,128},{80,144},{96,160},{112... | collective-permute-start | bytes 20 | tf_op jit(solution)/shard_map/ppermute | solution.py:47
  332.3 10.7 %collective-permute-start.67 = (f32[]{:T(128)}, f32[]{:T(128)}, u32[]{:S(2)}, u32[]{:S(2)}) collective-permute-start(f32[]{:T(128)} %add.497), channel_id=1, source_target_pairs={{0,2},{1,3},{2,0},{3,1},{4,6},{5,7},{6,4},{7,5},{8,10},{9,11},{10,... | collective-permute-start | bytes 20 | tf_op jit(solution)/shard_map/ppermute | solution.py:47
  344.3 9.5 %collective-permute-start.70 = (f32[]{:T(128)}, f32[]{:T(128)}, u32[]{:S(2)}, u32[]{:S(2)}) collective-permute-start(f32[]{:T(128)} %add.500), channel_id=1, source_target_pairs={{0,8},{1,9},{2,10},{3,11},{4,12},{5,13},{6,14},{7,15},{8,0},{9,1},... | collective-permute-start | bytes 20 | tf_op jit(solution)/shard_map/ppermute | solution.py:47
  (72 other events, 485.4 us)
